TPU v7x, 256 devices: a whole 4x4x8 slice. The times are simulated.
256 devices in a mesh: role: 2 (over core), dp: 16 (over x, y), tensor: 8 (over z).
Axes of the slice: x: 4, y: 4, z: 8, core: 2. Of those that a mesh axis runs over, the one named last changes fastest.
Arguments:
- queries: bfloat16 [1024, 128, 576], P(('dp', 'tensor'), 'role'), may hold values from -13 to 13
- latent_cache: bfloat16 [512, 1024, 576], P(('dp', 'tensor')), may hold values from -4 to 4
- new_latent: bfloat16 [1024, 576], P(('dp', 'tensor')), may hold values from -9 to 9
- cache_lengths: int32 [512], P(('dp', 'tensor')), may hold values from 2 to 1024
- value_proj: bfloat16 [128, 512, 128], P(('role', 'tensor')), may hold values from -1 to 1
- out_proj: bfloat16 [16384, 7168], P(('role', 'tensor'), 'dp'), may hold values from -0.046875 to 0.046875
- residual: bfloat16 [1024, 7168], P(('role', 'tensor'), 'dp'), may hold values from -68 to 68
- norm_gain: bfloat16 [7168], replicated, may hold values from 0.5 to 1.5
- routes: int32 [1024, 8], P(('role', 'tensor')), may hold values from 0 to 15, all different within a row; in each aligned block of 64 rows (0 to 63, 64 to 127, ...) at most 40 rows name the same one
- gate_values: float32 [1024, 8], P(('role', 'tensor')), may hold values from 0.2 to 0.8
- tenant_ids: int32 [1024], P(('role', 'tensor')), may hold values from 0 to 2
- expert_gate_weight: bfloat16 [16, 7168, 2048], P('dp', None, ('role', 'tensor')), may hold values from -0.0625 to 0.0625
- expert_up_weight: bfloat16 [16, 7168, 2048], P('dp', None, ('role', 'tensor')), may hold values from -0.0625 to 0.0625
- expert_down_weight: bfloat16 [16, 2048, 7168], P('dp', ('role', 'tensor')), may hold values from -0.125 to 0.125
- left_delta_factor: bfloat16 [3, 16, 2048, 64], P(None, 'dp', ('role', 'tensor')), may hold values from -0.125 to 0.125
- factor_right: bfloat16 [3, 16, 64, 7168], P(None, 'dp'), may hold values from -0.75 to 0.75
Outputs:
- mixed: bfloat16 [1024, 7168], P(('role', 'tensor'), 'dp')
Inputs may be any that keep to these rules, and one draw needn't show every extreme that they name: `routes`: in each aligned block of 64 tokens no expert is named by more than 40 of them.
All inputs are finite; a program needn't handle non-finite values.
Results may differ from a plain program's by a relative error of at most 0.008.
Values may be sent and summed in bfloat16 or wider, within the bound.
No kernel may reach another device: no remote copies, remote signals or barrier semaphores. Data moves between devices by JAX's collectives and lax.ppermute only.
A program may use at most 128 MiB of HBM per device.

v0:
```python
import jax
import jax.numpy as jnp
from jax import lax
from jax.sharding import PartitionSpec as P

LAT = 512
EXPERTS = 16
TEN = 3


SCORE_SCALE = 0.07216878364870323
NORM_EPS = 1e-06
MASKED = -1e30
RT = ("role", "tensor")


def rms_rows(input_rows, norm_gain):
    wide = input_rows.astype(jnp.float32)
    scale = lax.rsqrt(jnp.mean(wide * wide, axis=-1, keepdims=True) + NORM_EPS)
    return (wide * scale * norm_gain.astype(jnp.float32)).astype(jnp.bfloat16)


def slot_table(routes, expert, capacity):
    hit = jnp.any(routes == expert, axis=-1).astype(jnp.int32)
    earlier = jnp.cumsum(hit, axis=-1) - hit
    slot_ids = jnp.arange(capacity, dtype=jnp.int32)
    return (hit[..., None, :] > 0) & (earlier[..., None, :] == slot_ids[:, None])


def local(
    queries,
    latent_cache,
    new_latent,
    cache_lengths,
    value_proj,
    out_proj,
    residual,
    norm_gain,
    routes,
    gate_values,
    tenant_ids,
    expert_gate_weight,
    expert_up_weight,
    expert_down_weight,
    left_delta_factor,
    factor_right,
):
    n_slices = lax.axis_size(RT)
    slice_idx = lax.axis_index(RT)
    group_rows = residual.shape[0]
    capacity = 5 * group_rows // 8
    model_width = expert_down_weight.shape[2]
    col_width = model_width // n_slices

    expert = lax.axis_index("dp")
    labels = jnp.arange(EXPERTS, dtype=jnp.int32)
    table = slot_table(routes, labels[:, None, None], capacity)
    mine = lax.dynamic_index_in_dim(table, expert, 0, keepdims=False)
    mine_owner = jnp.sum(mine.astype(jnp.int32) * tenant_ids[None, :], axis=1)
    hidden_slice = expert_down_weight.shape[1]
    down_local = expert_down_weight[0].reshape(hidden_slice, n_slices, col_width)
    left_local = left_delta_factor[:, 0]
    tenants, _, rank = left_local.shape
    left_local = jnp.transpose(left_local, (1, 0, 2)).reshape(hidden_slice, 1, tenants * rank)
    left_local = jnp.broadcast_to(left_local, (hidden_slice, n_slices, tenants * rank))
    down_pack = jnp.concatenate([down_local, left_local], axis=2)
    down_pack = lax.all_to_all(down_pack, RT, split_axis=1, concat_axis=0, tiled=True)
    right_w = lax.dynamic_slice_in_dim(factor_right[:, 0], slice_idx * col_width, col_width, 2)

    seq_count, context, width = latent_cache.shape
    local_heads = queries.shape[1]
    paired = queries.reshape(seq_count, 2, local_heads, width)
    scores = (
        jnp.einsum("sqhd,spd->sqhp", paired, latent_cache, preferred_element_type=jnp.float32)
        * SCORE_SCALE
    )
    present = jnp.arange(context, dtype=jnp.int32)[None, :] < cache_lengths[:, None]
    scores = jnp.where(present[:, None, None, :], scores, MASKED)
    fresh_keys = new_latent.reshape(seq_count, 2, width)
    fresh = (
        jnp.einsum("sqhd,skd->sqhk", paired, fresh_keys, preferred_element_type=jnp.float32)
        * SCORE_SCALE
    )
    causal = jnp.arange(2)[:, None] >= jnp.arange(2)[None, :]
    fresh = jnp.where(causal[None, :, None, :], fresh, MASKED)
    top = jnp.maximum(jnp.max(scores, axis=3), jnp.max(fresh, axis=3))[..., None]
    weights = jnp.exp(scores - top)
    fresh_weights = jnp.exp(fresh - top)
    total = jnp.sum(weights, axis=3) + jnp.sum(fresh_weights, axis=3)
    summed = jnp.einsum(
        "sqhp,spd->sqhd",
        weights.astype(jnp.bfloat16),
        latent_cache[:, :, :LAT],
        preferred_element_type=jnp.float32,
    )
    summed = summed + jnp.einsum(
        "sqhk,skd->sqhd",
        fresh_weights.astype(jnp.bfloat16),
        fresh_keys[:, :, :LAT],
        preferred_element_type=jnp.float32,
    )
    attended = (
        (summed / total[..., None]).astype(jnp.bfloat16).reshape(seq_count * 2, local_heads, LAT)
    )
    by_head = lax.all_to_all(attended, "tensor", split_axis=1, concat_axis=0, tiled=True)
    head_values = jnp.einsum(
        "thl,hlv->thv", by_head, value_proj, preferred_element_type=jnp.float32
    ).astype(jnp.bfloat16)
    head_values = head_values.reshape(
        head_values.shape[0], head_values.shape[1] * head_values.shape[2]
    )
    all_values = lax.all_gather(head_values, "dp", axis=0, tiled=True)
    down_pack, all_values = lax.optimization_barrier((down_pack, all_values))
    partial = jnp.dot(all_values, out_proj, preferred_element_type=jnp.float32)
    half = partial.shape[0] // 2
    role_idx = lax.axis_index("role")
    keep = lax.dynamic_slice_in_dim(partial, role_idx * half, half, 0)
    give = lax.dynamic_slice_in_dim(partial, (1 - role_idx) * half, half, 0)
    partial = keep + lax.ppermute(give, "role", [(0, 1), (1, 0)])
    n_tensor = lax.axis_size("tensor")
    partial = partial.reshape(n_tensor, partial.shape[0] // n_tensor, partial.shape[1])
    partial = lax.all_to_all(partial, "tensor", split_axis=0, concat_axis=0, tiled=True)
    attention = jnp.sum(partial, axis=0)
    mixed_in = lax.optimization_barrier(
        (residual.astype(jnp.float32) + attention).astype(jnp.bfloat16)
    )

    full_rows = lax.all_gather(mixed_in.reshape(-1, 128), "dp", axis=0, tiled=True)
    full_rows = full_rows.reshape(-1, group_rows, mixed_in.shape[1])
    full_rows = jnp.transpose(full_rows, (1, 0, 2)).reshape(group_rows, model_width)
    normed = rms_rows(full_rows, norm_gain)
    picked = jnp.dot(
        mine.astype(jnp.bfloat16), normed, preferred_element_type=jnp.float32
    ).astype(jnp.bfloat16)
    collected_rows = lax.all_gather(picked, RT, axis=0, tiled=True)
    gate_scores = jnp.dot(collected_rows, expert_gate_weight[0], preferred_element_type=jnp.float32)
    upper_bound = jnp.dot(collected_rows, expert_up_weight[0], preferred_element_type=jnp.float32)
    hidden = (jax.nn.silu(gate_scores) * upper_bound).astype(jnp.bfloat16)

    lanes = hidden.shape[1]
    owner_block = jnp.zeros((8, lanes), jnp.bfloat16)
    owner_block = owner_block.at[0, :capacity].set(mine_owner.astype(jnp.bfloat16))
    hidden_ext = jnp.concatenate([hidden, owner_block], axis=0)
    gathered = lax.all_gather(hidden_ext, RT, axis=0, tiled=True)
    gathered = gathered.reshape(n_slices, hidden.shape[0] + 8, lanes)
    owners = gathered[:, hidden.shape[0], :capacity].astype(jnp.int32).reshape(n_slices * capacity)
    hidden_all = jnp.transpose(gathered[:, : hidden.shape[0]], (1, 0, 2)).reshape(hidden.shape[0], -1)
    down_pack = down_pack.reshape(n_slices * hidden_slice, col_width + tenants * rank)
    down_w = down_pack[:, :col_width]
    left_w = down_pack[:, col_width:].reshape(n_slices * hidden_slice, tenants, rank)
    base_output = jnp.dot(hidden_all, down_w, preferred_element_type=jnp.float32)
    owner_mask = (owners[:, None] == jnp.arange(TEN, dtype=jnp.int32)[None, :]).astype(jnp.float32)
    mixing = jnp.einsum(
        "sf,ftr->str", hidden_all, left_w, preferred_element_type=jnp.float32
    ) * owner_mask[:, :, None]
    delta = jnp.einsum(
        "str,trd->sd", mixing, right_w.astype(jnp.float32), precision=lax.Precision.HIGHEST
    )
    expert_out = (base_output - delta).astype(jnp.bfloat16)
    expert_out = expert_out.reshape(n_slices, capacity, col_width)
    by_group = lax.all_to_all(expert_out, RT, split_axis=0, concat_axis=0, tiled=True)
    by_expert = lax.all_to_all(by_group, "dp", split_axis=0, concat_axis=0, tiled=True)

    chosen = (routes[:, :, None] == labels[None, None, :]).astype(jnp.float32)
    gate_of = jnp.sum(gate_values[:, :, None] * chosen, axis=1)
    weighting = table.astype(jnp.float32) * gate_of.T[:, None, :]
    expert_part = jnp.einsum(
        "ecg,ecd->gd", weighting, by_expert.astype(jnp.float32), precision=lax.Precision.HIGHEST
    )
    return (mixed_in.astype(jnp.float32) + expert_part).astype(jnp.bfloat16)


def solution(mesh):
    placed = (
        P(("dp", "tensor"), "role", None),
        P(("dp", "tensor"), None, None),
        P(("dp", "tensor"), None),
        P(("dp", "tensor")),
        P(("role", "tensor"), None, None),
        P(("role", "tensor"), "dp"),
        P(("role", "tensor"), "dp"),
        P(),
        P(("role", "tensor"), None),
        P(("role", "tensor"), None),
        P(("role", "tensor")),
        P("dp", None, ("role", "tensor")),
        P("dp", None, ("role", "tensor")),
        P("dp", ("role", "tensor"), None),
        P(None, "dp", ("role", "tensor"), None),
        P(None, "dp", None, None),
    )
    return jax.shard_map(
        local, mesh=mesh, in_specs=placed, out_specs=P(("role", "tensor"), "dp"), check_vma=False
    )
```

profile of v0, /device:TPU:32, one launch (start us, length us, event | category | flops | bytes accessed | tf_op | source)
XLA Modules:
  0.0 375.9 jit_solution(17690924124041429193)
XLA Ops:
  6.5 0.9 iota_compare_fusion.4
  7.4 0.7 reshape.198
  8.2 3.9 %fusion.7 = (f32[4,2,64]{2,1,0:T(2,128)S(1)}, f32[4,2,64,1024]{3,2,1,0:T(8,128)S(1)}) fusion(pred[4,1024]{1,0:T(4,128)(4,1)S(1)} %iota_compare_fusion.4, bf16[4,2,64,576]{3,2,1,0:T(8,128)(2,1)} %bitcast.113, bf16[4,1024,576]{1,2,0:T(8,128)(2,1)} %param.19), kind=kOutput, calls=%fused_computation.13 | convolution fusion | flops 605552128 | bytes 7411712 | tf_op jit(solution)/shard_map/sqhd,spd->sqhp/dot_general | solution.py:74
  12.1 0.4 fusion.64
  12.5 2.5 fusion.2
  15.1 0.6 fusion.12
  15.7 0.1 copy-done.8
  15.8 1.6 fusion.17
  17.4 1.1 copy.68
  18.5 8.6 %all-to-all-start.1 = ((bf16[8,64,512]{2,0,1:T(8,128)(2,1)}), bf16[8,64,512]{2,0,1:T(8,128)(2,1)S(1)}, u32[]{:S(2)}, u32[]{:S(2)}) async-start(bf16[8,64,512]{2,0,1:T(8,128)(2,1)} %copy.68), calls=%async_computation.1 | async-start | bytes 1048576 | tf_op jit(solution)/shard_map/all_to_all | solution.py:105
  27.1 3.9 %copy.65 = bf16[1,128,7168]{1,2,0:T(8,128)(2,1)} copy(bf16[1,128,7168]{2,1,0:T(8,128)(2,1)} %param.31) | data formatting | bytes 3670016 | tf_op args[13]
  31.0 0.1 broadcast_in_dim.25
  31.1 3.2 pad_maximum_fusion
  34.3 8.8 %all-to-all-done.1 = bf16[8,64,512]{2,0,1:T(8,128)(2,1)S(1)} async-done(((bf16[8,64,512]{2,0,1:T(8,128)(2,1)}), bf16[8,64,512]{2,0,1:T(8,128)(2,1)S(1)}, u32[]{:S(2)}, u32[]{:S(2)}) %all-to-all-start.1) | async-done | bytes 524320 | tf_op jit(solution)/shard_map/all_to_all | solution.py:105
  43.1 5.7 %all-to-all-start = ((bf16[128,16,640]{0,2,1:T(8,128)(2,1)}), bf16[128,16,640]{0,2,1:T(8,128)(2,1)}, u32[]{:S(2)}, u32[]{:S(2)}) async-start(bf16[128,16,640]{0,2,1:T(8,128)(2,1)} %pad_maximum_fusion), calls=%async_computation | async-start | bytes 5242880 | tf_op jit(solution)/shard_map/all_to_all | solution.py:67
  48.7 0.0 all-gather.4.cloned.1.call-start
  48.8 1.5 fusion.25
  50.3 0.7 copy.90
  51.0 0.0 all-gather.4.cloned.1.call-update
  51.0 57.5 %all-to-all-done = bf16[128,16,640]{0,2,1:T(8,128)(2,1)} async-done(((bf16[128,16,640]{0,2,1:T(8,128)(2,1)}), bf16[128,16,640]{0,2,1:T(8,128)(2,1)}, u32[]{:S(2)}, u32[]{:S(2)}) %all-to-all-start) | async-done | bytes 2621472 | tf_op jit(solution)/shard_map/all_to_all | solution.py:67
  108.5 4.4 %copy.66 = bf16[16,128,1,640]{3,1,0,2:T(8,128)(2,1)} copy(bf16[16,128,1,640]{1,3,0,2:T(8,128)(2,1)} %bitcast.5) | data formatting | bytes 5242880 | tf_op jit(solution)/shard_map/all_to_all | solution.py:67
  112.9 3.0 fusion.65
  115.9 1.2 copy-done.4
  117.2 1.0 constant_dynamic-slice_fusion
  118.2 0.3 collective-permute-start
  118.5 2.5 collective-permute-done
  121.0 2.6 dynamic-slice_add_fusion
  123.6 2.5 copy.71
  126.1 5.6 %all-to-all-start.2 = ((f32[8,64,448]{2,1,0:T(8,128)}), f32[8,64,448]{2,1,0:T(8,128)}, u32[]{:S(2)}, u32[]{:S(2)}) async-start(f32[8,64,448]{2,1,0:T(8,128)} %bitcast.104), calls=%async_computation.2 | async-start | bytes 2097152 | tf_op jit(solution)/shard_map/all_to_all | solution.py:122
  131.8 0.2 reduce_window_sum.11
  132.0 0.1 reshape.195
  132.1 0.1 fusion.41
  132.2 27.2 %all-to-all-done.2 = f32[8,64,448]{2,1,0:T(8,128)} async-done(((f32[8,64,448]{2,1,0:T(8,128)}), f32[8,64,448]{2,1,0:T(8,128)}, u32[]{:S(2)}, u32[]{:S(2)}) %all-to-all-start.2) | async-done | bytes 917536 | tf_op jit(solution)/shard_map/all_to_all | solution.py:122
  159.4 1.3 reduce_sum.56
  160.8 0.1 reshape.188
  160.9 26.8 %all_gather.13 = bf16[3584,128]{1,0:T(8,128)(2,1)} all-gather(bf16[224,128]{1,0:T(8,128)(2,1)S(1)} %reshape.188), channel_id=1, replica_groups=mesh['role'=2,'dp'=16,'tensor'=8] {'dp'}, dimensions={0}, use_global_device_ids=true | all-gather | bytes 974848 | tf_op jit(solution)/shard_map/all_gather | solution.py:128
  187.7 2.8 reshape.194
  190.5 2.1 multiply_reduce_fusion
  192.6 0.1 copy-done.1
  192.8 0.4 fusion.29
  193.2 1.5 copy.72
  194.7 2.9 convert_element_type.116
  197.6 2.3 convolution_convert_fusion
  199.9 0.2 all-gather.8.cloned.1.call-start
  200.2 0.1 select_reduce_fusion.1
  200.3 52.9 %all-gather.6.cloned.1.call-done = bf16[640,7168]{1,0:T(8,128)(2,1)} async-done(((bf16[40,7168]{1,0:T(8,128)(2,1)}), bf16[640,7168]{1,0:T(8,128)(2,1)}) %all-gather.6.cloned.1.call-update) | async-done | bytes 9175056 | tf_op jit(solution)/shard_map/all_gather | solution.py:135
  253.2 6.8 %fusion.10 = f32[640,128]{1,0:T(8,128)S(1)} fusion(bf16[640,7168]{1,0:T(8,128)(2,1)} %all-gather.6.cloned.1.call-done, bf16[1,7168,128]{2,1,0:T(8,128)(2,1)} %param.29), kind=kOutput, calls=%fused_computation.16 | convolution fusion | flops 1174405120 | bytes 11337728 | tf_op jit(solution)/shard_map/dot_general | solution.py:136
  260.0 0.4 copy-done.14
  260.5 2.5 fusion.21
  263.0 0.7 fusion.45
  263.7 0.0 all-gather.8.cloned.1.call-update
  263.7 40.4 %all-gather.8.cloned.1.call-done = bf16[10368,128]{1,0:T(8,128)(2,1)} async-done(((bf16[648,128]{1,0:T(8,128)(2,1)}), bf16[10368,128]{1,0:T(8,128)(2,1)}) %all-gather.8.cloned.1.call-update) | async-done | bytes 2654224 | tf_op jit(solution)/shard_map/all_gather | solution.py:144
  304.1 3.5 slice.41
  307.6 4.4 %copy.83 = bf16[16,640,128]{1,2,0:T(8,128)(2,1)} copy(bf16[16,640,128]{2,1,0:T(8,128)(2,1)} %slice.41) | data formatting | bytes 5242880
  312.0 5.2 %fusion.5 = f32[640,448]{0,1:T(8,128)} fusion(bf16[640,2048]{0,1:T(8,128)(2,1)} %bitcast.107, bf16[2048,640]{1,0:T(8,128)(2,1)} %bitcast.105), kind=kOutput, calls=%fused_computation.7 | convolution fusion | flops 1174405120 | bytes 5865472 | tf_op jit(solution)/shard_map/dot_general | solution.py:151
  317.2 2.4 fusion.30
  319.6 0.8 fusion.53
  320.4 0.1 reshape.196
  320.5 2.9 fusion.16
  323.4 1.3 copy.76
  324.7 24.5 %all_to_all.51 = bf16[16,40,448]{2,1,0:T(8,128)(2,1)} all-to-all(bf16[16,40,448]{2,1,0:T(8,128)(2,1)S(1)} %bitcast.109), channel_id=1, replica_groups=mesh['role'=2,'dp'=16,'tensor'=8] {'role','tensor'}, dimensions={0} | all-to-all | bytes 1146880 | tf_op jit(solution)/shard_map/all_to_all | solution.py:161
  349.2 6.8 %all-to-all-start.4 = ((bf16[16,40,448]{2,1,0:T(8,128)(2,1)}), bf16[16,40,448]{2,1,0:T(8,128)(2,1)S(1)}, u32[]{:S(2)}, u32[]{:S(2)}) async-start(bf16[16,40,448]{2,1,0:T(8,128)(2,1)} %all_to_all.51), calls=%async_computation.4 | async-start | bytes 1310720 | tf_op jit(solution)/shard_map/all_to_all | solution.py:162
  356.1 12.1 %all-to-all-done.4 = bf16[16,40,448]{2,1,0:T(8,128)(2,1)S(1)} async-done(((bf16[16,40,448]{2,1,0:T(8,128)(2,1)}), bf16[16,40,448]{2,1,0:T(8,128)(2,1)S(1)}, u32[]{:S(2)}, u32[]{:S(2)}) %all-to-all-start.4) | async-done | bytes 573472 | tf_op jit(solution)/shard_map/all_to_all | solution.py:162
  368.2 1.1 fusion.26
  (42 shorter events, 0.2 us)
Async XLA Ops:
  6.5 313.9 %copy-start = (bf16[3,1,64,7168]{3,2,1,0:T(8,128)(2,1)S(1)}, bf16[3,1,64,7168]{3,2,1,0:T(8,128)(2,1)}, u32[]{:S(2)}) copy-start(bf16[3,1,64,7168]{3,2,1,0:T(8,128)(2,1)} %param.33) | copy-start | bytes 8257540
  8.1 3.9 %copy-start.5 = (bf16[8,64,576]{2,1,0:T(8,128)(2,1)S(1)}, bf16[8,64,576]{2,1,0:T(8,128)(2,1)}, u32[]{:S(2)}) copy-start(bf16[8,64,576]{2,1,0:T(8,128)(2,1)} %param.18) | copy-start | bytes 1769476
  8.1 4.4 %copy-start.2 = (bf16[4,1024,576]{1,2,0:T(8,128)(2,1)S(1)}, bf16[4,1024,576]{1,2,0:T(8,128)(2,1)}, u32[]{:S(2)}) copy-start(bf16[4,1024,576]{1,2,0:T(8,128)(2,1)} %param.19) | copy-start | bytes 14155780
  15.1 0.7 copy-start.8
  18.5 24.6 %all-to-all-start.1 = ((bf16[8,64,512]{2,0,1:T(8,128)(2,1)}), bf16[8,64,512]{2,0,1:T(8,128)(2,1)S(1)}, u32[]{:S(2)}, u32[]{:S(2)}) async-start(bf16[8,64,512]{2,0,1:T(8,128)(2,1)} %copy.68), calls=%async_computation.1 | async-start | bytes 1048576 | tf_op jit(solution)/shard_map/all_to_all | solution.py:105
  27.1 3.9 %copy-start.7 = (bf16[3,1,128,64]{2,3,1,0:T(8,128)(2,1)S(1)}, bf16[3,1,128,64]{2,3,1,0:T(8,128)(2,1)}, u32[]{:S(2)}) copy-start(bf16[3,1,128,64]{2,3,1,0:T(8,128)(2,1)} %param.32) | copy-start | bytes 147460
  43.1 65.4 %all-to-all-start = ((bf16[128,16,640]{0,2,1:T(8,128)(2,1)}), bf16[128,16,640]{0,2,1:T(8,128)(2,1)}, u32[]{:S(2)}, u32[]{:S(2)}) async-start(bf16[128,16,640]{0,2,1:T(8,128)(2,1)} %pad_maximum_fusion), calls=%async_computation | async-start | bytes 5242880 | tf_op jit(solution)/shard_map/all_to_all | solution.py:67
  48.7 64.2 %all-gather.4.cloned.1.call-start = ((), (), s32[]{:S(2)}) async-start(), calls=%async_computation.5 | async-start | bytes 2228224 | tf_op jit(solution)/shard_map/all_gather | solution.py:112
  115.9 1.3 copy-start.4
  118.2 2.8 collective-permute-start
  123.6 8.2 %copy-start.9 = (s32[64,8]{0,1:T(8,128)S(1)}, s32[64,8]{0,1:T(8,128)}, u32[]{:S(2)}) copy-start(s32[64,8]{0,1:T(8,128)} %param.26) | copy-start | bytes 6148
  123.6 8.4 %copy-start.10 = (bf16[7168]{0:T(1024)(128)(2,1)S(1)}, bf16[7168]{0:T(1024)(128)(2,1)}, u32[]{:S(2)}) copy-start(bf16[7168]{0:T(1024)(128)(2,1)} %param.25) | copy-start | bytes 43012
  126.1 34.6 %copy-start.6 = (bf16[64,448]{1,0:T(8,128)(2,1)S(1)}, bf16[64,448]{1,0:T(8,128)(2,1)}, u32[]{:S(2)}) copy-start(bf16[64,448]{1,0:T(8,128)(2,1)} %param.24) | copy-start | bytes 172036
  126.1 33.3 %all-to-all-start.2 = ((f32[8,64,448]{2,1,0:T(8,128)}), f32[8,64,448]{2,1,0:T(8,128)}, u32[]{:S(2)}, u32[]{:S(2)}) async-start(f32[8,64,448]{2,1,0:T(8,128)} %bitcast.104), calls=%async_computation.2 | async-start | bytes 2097152 | tf_op jit(solution)/shard_map/all_to_all | solution.py:122
  131.7 121.5 %all-gather.6.cloned.1.call-start = ((), (), s32[]{:S(2)}) async-start(), calls=%async_computation.6 | async-start | bytes 9748480 | tf_op jit(solution)/shard_map/all_gather | solution.py:135
  190.5 2.2 copy-start.1
  194.7 5.5 %copy-start.12 = (s32[64]{0:T(128)S(1)}, s32[64]{0:T(128)}, u32[]{:S(2)}) copy-start(s32[64]{0:T(128)} %param.28) | copy-start | bytes 772
  199.9 104.2 %all-gather.8.cloned.1.call-start = ((), (), s32[]{:S(2)}) async-start(), calls=%async_computation.7 | async-start | bytes 2820096 | tf_op jit(solution)/shard_map/all_gather | solution.py:144
  253.2 6.8 %copy-start.13 = (bf16[640,7168]{1,0:T(8,128)(2,1)S(1)}, bf16[640,7168]{1,0:T(8,128)(2,1)}, u32[]{:S(2)}) copy-start(bf16[640,7168]{1,0:T(8,128)(2,1)} %all-gather.6.cloned.1.call-done) | copy-start | bytes 27525124
  253.2 7.2 %copy-start.14 = (bf16[1,7168,128]{2,1,0:T(8,128)(2,1)S(1)}, bf16[1,7168,128]{2,1,0:T(8,128)(2,1)}, u32[]{:S(2)}) copy-start(bf16[1,7168,128]{2,1,0:T(8,128)(2,1)} %param.30) | copy-start | bytes 5505028
  312.0 5.2 %copy-start.3 = (bf16[16,640,128]{1,2,0:T(8,128)(2,1)S(1)}, bf16[16,640,128]{1,2,0:T(8,128)(2,1)}, u32[]{:S(2)}) copy-start(bf16[16,640,128]{1,2,0:T(8,128)(2,1)} %copy.83) | copy-start | bytes 7864324
  323.4 32.7 %copy-start.11 = (f32[64,8]{0,1:T(8,128)S(1)}, f32[64,8]{0,1:T(8,128)}, u32[]{:S(2)}) copy-start(f32[64,8]{0,1:T(8,128)} %param.27) | copy-start | bytes 6148
  349.2 19.0 %all-to-all-start.4 = ((bf16[16,40,448]{2,1,0:T(8,128)(2,1)}), bf16[16,40,448]{2,1,0:T(8,128)(2,1)S(1)}, u32[]{:S(2)}, u32[]{:S(2)}) async-start(bf16[16,40,448]{2,1,0:T(8,128)(2,1)} %all_to_all.51), calls=%async_computation.4 | async-start | bytes 1310720 | tf_op jit(solution)/shard_map/all_to_all | solution.py:162
Sparse Core Ops, SparseCore 0:
  52.0 51.1 all-gather.3
  200.1 53.1 all-gather.5
  263.8 40.2 all-gather.7
where the time goes:
time: 377 us; the launch traced here: 376 us
  waiting for transfers between devices  202 us (54%)
  blocking collectives  51.3 us (14%)
  matrix products  36.1 us (10%)
  local copies, waits for them, and re-layouts  33.2 us (9%)
  starting transfers between devices  27.3 us (7%)
  between operations  13.4 us (4%)
  other arithmetic  13 us (3%)
    all_to_all x1, waiting for transfers between devices, local(): lax.all_to_all(down_pack, RT, split_axis=1, concat_axis=0, tiled=True)  57.5 us
    all_gather x1, waiting for transfers between devices, local(): collected_rows = lax.all_gather(picked, RT, axis=0, tiled=True)  52.9 us
    all_gather x1, waiting for transfers between devices, local(): gathered = lax.all_gather(hidden_ext, RT, axis=0, tiled=True)  40.4 us
    all_to_all x1, waiting for transfers between devices, local(): lax.all_to_all(partial, 'tensor', split_axis=0, concat_axis=0, tiled=True)  27.2 us
    all_gather x1, blocking collectives, local(): lax.all_gather(mixed_in.reshape(-1, 128), 'dp', axis=0, tiled=True)  26.8 us
    all_to_all x1, blocking collectives, local(): lax.all_to_all(expert_out, RT, split_axis=0, concat_axis=0, tiled=True)  24.5 us
    all_to_all x1, waiting for transfers between devices, local(): lax.all_to_all(by_group, 'dp', split_axis=0, concat_axis=0, tiled=True)  12.1 us
    unnamed x32, local copies, waits for them, and re-layouts  10.3 us
  transfers between devices with their start and end apart: 8, of which 7 were waited for; matrix products, arithmetic and copies ran while one was open for 4% of the time, Pallas kernels for 0%

commit v1 on v0

--- a/solution.py
+++ b/solution.py
@@ -64,6 +64,11 @@
     left_local = jnp.transpose(left_local, (1, 0, 2)).reshape(hidden_slice, 1, tenants * rank)
     left_local = jnp.broadcast_to(left_local, (hidden_slice, n_slices, tenants * rank))
     down_pack = jnp.concatenate([down_local, left_local], axis=2)
+    pack_width = down_pack.shape[2]
+    info = mine_owner.astype(jnp.bfloat16)
+    info_rows = jnp.zeros((8, pack_width), jnp.bfloat16).at[0, : info.shape[0]].set(info)
+    info_rows = jnp.broadcast_to(info_rows[:, None, :], (8, n_slices, pack_width))
+    down_pack = jnp.concatenate([down_pack, info_rows], axis=0)
     down_pack = lax.all_to_all(down_pack, RT, split_axis=1, concat_axis=0, tiled=True)
     right_w = lax.dynamic_slice_in_dim(factor_right[:, 0], slice_idx * col_width, col_width, 2)
 
@@ -110,7 +115,12 @@
         head_values.shape[0], head_values.shape[1] * head_values.shape[2]
     )
     all_values = lax.all_gather(head_values, "dp", axis=0, tiled=True)
-    down_pack, all_values = lax.optimization_barrier((down_pack, all_values))
+    down_pack = down_pack.reshape(n_slices, hidden_slice + 8, pack_width)
+    owners = down_pack[:, hidden_slice, :capacity].astype(jnp.int32).reshape(n_slices * capacity)
+    down_pack = down_pack[:, :hidden_slice].reshape(n_slices * hidden_slice, pack_width)
+    down_w = down_pack[:, :col_width]
+    left_w = down_pack[:, col_width:].reshape(n_slices * hidden_slice, tenants, rank)
+    down_w, left_w, owners, all_values = lax.optimization_barrier((down_w, left_w, owners, all_values))
     partial = jnp.dot(all_values, out_proj, preferred_element_type=jnp.float32)
     half = partial.shape[0] // 2
     role_idx = lax.axis_index("role")
@@ -125,7 +135,7 @@
         (residual.astype(jnp.float32) + attention).astype(jnp.bfloat16)
     )
 
-    full_rows = lax.all_gather(mixed_in.reshape(-1, 128), "dp", axis=0, tiled=True)
+    full_rows = lax.all_gather(mixed_in, "dp", axis=0, tiled=True)
     full_rows = full_rows.reshape(-1, group_rows, mixed_in.shape[1])
     full_rows = jnp.transpose(full_rows, (1, 0, 2)).reshape(group_rows, model_width)
     normed = rms_rows(full_rows, norm_gain)
@@ -137,17 +147,8 @@
     upper_bound = jnp.dot(collected_rows, expert_up_weight[0], preferred_element_type=jnp.float32)
     hidden = (jax.nn.silu(gate_scores) * upper_bound).astype(jnp.bfloat16)
 
-    lanes = hidden.shape[1]
-    owner_block = jnp.zeros((8, lanes), jnp.bfloat16)
-    owner_block = owner_block.at[0, :capacity].set(mine_owner.astype(jnp.bfloat16))
-    hidden_ext = jnp.concatenate([hidden, owner_block], axis=0)
-    gathered = lax.all_gather(hidden_ext, RT, axis=0, tiled=True)
-    gathered = gathered.reshape(n_slices, hidden.shape[0] + 8, lanes)
-    owners = gathered[:, hidden.shape[0], :capacity].astype(jnp.int32).reshape(n_slices * capacity)
-    hidden_all = jnp.transpose(gathered[:, : hidden.shape[0]], (1, 0, 2)).reshape(hidden.shape[0], -1)
-    down_pack = down_pack.reshape(n_slices * hidden_slice, col_width + tenants * rank)
-    down_w = down_pack[:, :col_width]
-    left_w = down_pack[:, col_width:].reshape(n_slices * hidden_slice, tenants, rank)
+    gathered = lax.all_gather(hidden, RT, axis=0, tiled=False)
+    hidden_all = jnp.transpose(gathered, (1, 0, 2)).reshape(hidden.shape[0], -1)
     base_output = jnp.dot(hidden_all, down_w, preferred_element_type=jnp.float32)
     owner_mask = (owners[:, None] == jnp.arange(TEN, dtype=jnp.int32)[None, :]).astype(jnp.float32)
     mixing = jnp.einsum(

time: 377 us -> 376 us (level)
  waiting for transfers between devices: 202 us -> 195 us
  local copies, waits for them, and re-layouts: 33.2 us -> 38 us
    all_to_all x1, waiting for transfers between devices: 8.79 us -> 0.01 us  [local(): lax.all_to_all(attended, 'tensor', split_axis=1, concat_axis=0, tiled=True)]
    concatenate x0 -> x2, local copies, waits for them, and re-layouts: none -> 6.25 us  [the longest x1 6.22 us: local(): down_pack = jnp.concatenate([down_pack, info_rows], axis=0)]
    all_to_all x1 -> x0, local copies, waits for them, and re-layouts: 4.39 us -> none  [local(): lax.all_to_all(down_pack, RT, split_axis=1, concat_axis=0, tiled=True)]
    all_gather x0 -> x1, local copies, waits for them, and re-layouts: none -> 4.38 us  [local(): gathered = lax.all_gather(hidden, RT, axis=0, tiled=False)]
    unnamed x32 -> x48, local copies, waits for them, and re-layouts: 10.3 us -> 8.09 us
  transfers between devices with their start and end apart: 8 -> 8, of which waited for: 7 -> 6; matrix products, arithmetic and copies ran while one was open for 4% -> 7% of each run, Pallas kernels for 0% -> 0%
where the time goes in v1:
time: 376 us; the launch traced here: 374 us
  waiting for transfers between devices  195 us (52%)
  blocking collectives  50.2 us (13%)
  local copies, waits for them, and re-layouts  38 us (10%)
  matrix products  33.9 us (9%)
  starting transfers between devices  28.7 us (8%)
  other arithmetic  15.3 us (4%)
  between operations  13.5 us (4%)
    all_to_all x1, waiting for transfers between devices, local(): lax.all_to_all(down_pack, RT, split_axis=1, concat_axis=0, tiled=True)  60.8 us
    all_gather x1, waiting for transfers between devices, local(): collected_rows = lax.all_gather(picked, RT, axis=0, tiled=True)  53.1 us
    all_gather x1, waiting for transfers between devices, local(): gathered = lax.all_gather(hidden, RT, axis=0, tiled=False)  39.7 us
    all_to_all x1, waiting for transfers between devices, local(): lax.all_to_all(partial, 'tensor', split_axis=0, concat_axis=0, tiled=True)  26.3 us
    all_gather x1, blocking collectives, local(): full_rows = lax.all_gather(mixed_in, 'dp', axis=0, tiled=True)  25.6 us
    all_to_all x1, blocking collectives, local(): lax.all_to_all(expert_out, RT, split_axis=0, concat_axis=0, tiled=True)  24.5 us
    all_to_all x1, waiting for transfers between devices, local(): lax.all_to_all(by_group, 'dp', split_axis=0, concat_axis=0, tiled=True)  12.1 us
    all_to_all x1, starting transfers between devices, local(): lax.all_to_all(attended, 'tensor', split_axis=1, concat_axis=0, tiled=True)  8.57 us
  transfers between devices with their start and end apart: 8, of which 6 were waited for; matrix products, arithmetic and copies ran while one was open for 7% of the time, Pallas kernels for 0%

profile of v1, /device:TPU:32, one launch (start us, length us, event | category | flops | bytes accessed | tf_op | source)
XLA Modules:
  0.0 374.2 jit_solution(17189568847510007043)
XLA Ops:
  6.5 0.9 iota_compare_fusion.3
  7.4 0.7 reshape.200
  8.2 3.9 %fusion.7 = (f32[4,2,64]{2,1,0:T(2,128)S(1)}, f32[4,2,64,1024]{3,2,1,0:T(8,128)S(1)}) fusion(pred[4,1024]{1,0:T(4,128)(4,1)S(1)} %iota_compare_fusion.3, bf16[4,2,64,576]{3,2,1,0:T(8,128)(2,1)} %bitcast.121, bf16[4,1024,576]{1,2,0:T(8,128)(2,1)} %param.19), kind=kOutput, calls=%fused_computation.13 | convolution fusion | flops 605552128 | bytes 7411712 | tf_op jit(solution)/shard_map/sqhd,spd->sqhp/dot_general | solution.py:79
  12.1 0.4 fusion.60
  12.6 0.6 fusion.12
  13.2 2.5 fusion.2
  15.8 1.6 fusion.17
  17.4 1.1 copy.74
  18.5 8.6 %all-to-all-start.1 = ((bf16[8,64,512]{2,0,1:T(8,128)(2,1)}), bf16[8,64,512]{2,0,1:T(8,128)(2,1)S(1)}, u32[]{:S(2)}, u32[]{:S(2)}) async-start(bf16[8,64,512]{2,0,1:T(8,128)(2,1)} %copy.74), calls=%async_computation.1 | async-start | bytes 1048576 | tf_op jit(solution)/shard_map/all_to_all | solution.py:110
  27.2 0.2 reduce_window_sum.11
  27.4 0.1 fusion.38
  27.5 0.6 copy-done.8
  28.1 0.1 select_reduce_fusion.1
  28.2 0.1 copy.88
  28.3 3.9 %copy.69 = bf16[1,128,7168]{1,2,0:T(8,128)(2,1)} copy(bf16[1,128,7168]{2,1,0:T(8,128)(2,1)} %param.31) | data formatting | bytes 3670016 | tf_op args[13]
  32.3 0.5 broadcast_in_dim.28
  32.8 0.9 copy-done.2
  33.7 3.5 pad_maximum_fusion
  37.2 6.2 %copy.71 = bf16[136,16,640]{2,0,1:T(8,128)(2,1)} copy(bf16[136,16,640]{0,2,1:T(8,128)(2,1)} %pad_maximum_fusion) | data formatting | bytes 5570560 | tf_op jit(solution)/shard_map/concatenate | solution.py:71
  43.4 7.2 %all-to-all-start = ((bf16[136,16,640]{2,0,1:T(8,128)(2,1)}), bf16[136,16,640]{2,0,1:T(8,128)(2,1)}, u32[]{:S(2)}, u32[]{:S(2)}) async-start(bf16[136,16,640]{2,0,1:T(8,128)(2,1)} %copy.71), calls=%async_computation | async-start | bytes 5570560 | tf_op jit(solution)/shard_map/all_to_all | solution.py:72
  50.7 1.5 fusion.25
  52.3 0.7 copy.102
  53.0 60.8 %all-to-all-done = bf16[136,16,640]{2,0,1:T(8,128)(2,1)} async-done(((bf16[136,16,640]{2,0,1:T(8,128)(2,1)}), bf16[136,16,640]{2,0,1:T(8,128)(2,1)}, u32[]{:S(2)}, u32[]{:S(2)}) %all-to-all-start) | async-done | bytes 2785312 | tf_op jit(solution)/shard_map/all_to_all | solution.py:72
  113.8 2.0 slice.40
  115.8 1.5 slice.41
  117.3 1.4 slice.42
  118.7 1.4 copy.72
  120.1 0.8 fusion.49
  120.9 0.7 reshape.195
  121.6 3.0 fusion.61
  124.6 1.3 copy-done.3
  125.8 1.0 constant_dynamic-slice_fusion
  126.9 0.4 collective-permute-start
  127.3 2.4 collective-permute-done
  129.7 2.6 dynamic-slice_add_fusion
  132.3 2.5 copy.77
  134.8 5.6 %all-to-all-start.2 = ((f32[8,64,448]{2,1,0:T(8,128)}), f32[8,64,448]{2,1,0:T(8,128)}, u32[]{:S(2)}, u32[]{:S(2)}) async-start(f32[8,64,448]{2,1,0:T(8,128)} %bitcast.116), calls=%async_computation.2 | async-start | bytes 2097152 | tf_op jit(solution)/shard_map/all_to_all | solution.py:132
  140.4 1.4 reshape.197
  141.8 26.3 %all-to-all-done.2 = f32[8,64,448]{2,1,0:T(8,128)} async-done(((f32[8,64,448]{2,1,0:T(8,128)}), f32[8,64,448]{2,1,0:T(8,128)}, u32[]{:S(2)}, u32[]{:S(2)}) %all-to-all-start.2) | async-done | bytes 917536 | tf_op jit(solution)/shard_map/all_to_all | solution.py:132
  168.1 2.0 reduce_sum.57
  170.1 0.9 add_convert_fusion
  171.0 0.6 copy-done.5
  171.6 25.6 %all_gather.16 = bf16[1024,448]{1,0:T(8,128)(2,1)S(1)} all-gather(bf16[64,448]{1,0:T(8,128)(2,1)S(1)} %add_convert_fusion), channel_id=1, replica_groups=mesh['role'=2,'dp'=16,'tensor'=8] {'dp'}, dimensions={0}, use_global_device_ids=true | all-gather | bytes 974848 | tf_op jit(solution)/shard_map/all_gather | solution.py:138
  197.3 0.3 bitcast_convert_fusion
  197.6 0.3 multiply_reduce_fusion
  197.9 0.1 copy-done.7
  198.0 2.3 fusion.29
  200.4 2.9 convert_element_type.117
  203.3 2.3 convolution_convert_fusion
  205.7 53.1 %all-gather.7.cloned.1.call-done = bf16[640,7168]{1,0:T(8,128)(2,1)} async-done(((bf16[40,7168]{1,0:T(8,128)(2,1)}), bf16[640,7168]{1,0:T(8,128)(2,1)}) %all-gather.7.cloned.1.call-update) | async-done | bytes 9175056 | tf_op jit(solution)/shard_map/all_gather | solution.py:145
  258.8 6.8 %fusion.10 = f32[640,128]{1,0:T(8,128)S(1)} fusion(bf16[640,7168]{1,0:T(8,128)(2,1)} %all-gather.7.cloned.1.call-done, bf16[1,7168,128]{2,1,0:T(8,128)(2,1)} %param.29), kind=kOutput, calls=%fused_computation.16 | convolution fusion | flops 1174405120 | bytes 11337728 | tf_op jit(solution)/shard_map/dot_general | solution.py:146
  265.6 0.4 copy-done.20
  266.0 3.2 fusion.21
  269.3 0.6 fusion.48
  269.9 39.7 %all-gather.9.cloned.1.call-done = bf16[10240,128]{1,0:T(8,128)(2,1)} async-done(((bf16[640,128]{1,0:T(8,128)(2,1)}), bf16[10240,128]{1,0:T(8,128)(2,1)}) %all-gather.9.cloned.1.call-update) | async-done | bytes 2621456 | tf_op jit(solution)/shard_map/all_gather | solution.py:150
  309.6 4.4 %copy.79 = bf16[16,640,128]{1,2,0:T(8,128)(2,1)} copy(bf16[16,640,128]{2,1,0:T(8,128)(2,1)} %bitcast.117) | data formatting | bytes 5242880 | tf_op jit(solution)/shard_map/all_gather | solution.py:150
  314.0 2.7 fusion.63
  316.7 3.3 fusion.62
  320.0 1.7 fusion.16
  321.7 1.3 copy.81
  323.0 24.5 %all_to_all.48 = bf16[16,40,448]{2,1,0:T(8,128)(2,1)} all-to-all(bf16[16,40,448]{2,1,0:T(8,128)(2,1)S(1)} %bitcast.118), channel_id=1, replica_groups=mesh['role'=2,'dp'=16,'tensor'=8] {'role','tensor'}, dimensions={0} | all-to-all | bytes 1146880 | tf_op jit(solution)/shard_map/all_to_all | solution.py:162
  347.6 6.8 %all-to-all-start.4 = ((bf16[16,40,448]{2,1,0:T(8,128)(2,1)}), bf16[16,40,448]{2,1,0:T(8,128)(2,1)S(1)}, u32[]{:S(2)}, u32[]{:S(2)}) async-start(bf16[16,40,448]{2,1,0:T(8,128)(2,1)} %all_to_all.48), calls=%async_computation.4 | async-start | bytes 1310720 | tf_op jit(solution)/shard_map/all_to_all | solution.py:163
  354.4 12.1 %all-to-all-done.4 = bf16[16,40,448]{2,1,0:T(8,128)(2,1)S(1)} async-done(((bf16[16,40,448]{2,1,0:T(8,128)(2,1)}), bf16[16,40,448]{2,1,0:T(8,128)(2,1)S(1)}, u32[]{:S(2)}, u32[]{:S(2)}) %all-to-all-start.4) | async-done | bytes 573472 | tf_op jit(solution)/shard_map/all_to_all | solution.py:163
  366.6 1.1 fusion.26
  (62 shorter events, 0.4 us)
Async XLA Ops:
  6.5 313.4 %copy-start = (bf16[3,1,64,7168]{3,2,1,0:T(8,128)(2,1)S(1)}, bf16[3,1,64,7168]{3,2,1,0:T(8,128)(2,1)}, u32[]{:S(2)}) copy-start(bf16[3,1,64,7168]{3,2,1,0:T(8,128)(2,1)} %param.33) | copy-start | bytes 8257540
  8.1 5.0 %slice-start = ((s8[4718592]{0:T(1024)(128)(4,1)}), s8[4194304]{0:T(1024)(128)(4,1)S(1)}, s32[]{:S(2)}) async-start(s8[4718592]{0:T(1024)(128)(4,1)} %bitcast.114), calls=%async_computation.8 | async-start | bytes 8388608
  8.1 4.0 %copy-start.4 = (bf16[8,64,576]{2,1,0:T(8,128)(2,1)S(1)}, bf16[8,64,576]{2,1,0:T(8,128)(2,1)}, u32[]{:S(2)}) copy-start(bf16[8,64,576]{2,1,0:T(8,128)(2,1)} %param.18) | copy-start | bytes 1769476
  8.2 5.0 %slice-start.1 = ((s8[4718592]{0:T(1024)(128)(4,1)}), s8[524288]{0:T(1024)(128)(4,1)S(1)}, s32[]{:S(2)}) async-start(s8[4718592]{0:T(1024)(128)(4,1)} %bitcast.114), calls=%async_computation.9 | async-start | bytes 1048576
  13.2 2.5 copy-start.11
  15.8 11.3 %copy-start.15 = (s32[64,8]{0,1:T(8,128)S(1)}, s32[64,8]{0,1:T(8,128)}, u32[]{:S(2)}) copy-start(s32[64,8]{0,1:T(8,128)} %param.26) | copy-start | bytes 6148
  17.4 10.7 %copy-start.18 = (s32[64]{0:T(128)S(1)}, s32[64]{0:T(128)}, u32[]{:S(2)}) copy-start(s32[64]{0:T(128)} %param.28) | copy-start | bytes 772
  18.5 24.9 %all-to-all-start.1 = ((bf16[8,64,512]{2,0,1:T(8,128)(2,1)}), bf16[8,64,512]{2,0,1:T(8,128)(2,1)S(1)}, u32[]{:S(2)}, u32[]{:S(2)}) async-start(bf16[8,64,512]{2,0,1:T(8,128)(2,1)} %copy.74), calls=%async_computation.1 | async-start | bytes 1048576 | tf_op jit(solution)/shard_map/all_to_all | solution.py:110
  27.1 5.2 %copy-start.9 = (bf16[3,1,128,64]{2,3,1,0:T(8,128)(2,1)S(1)}, bf16[3,1,128,64]{2,3,1,0:T(8,128)(2,1)}, u32[]{:S(2)}) copy-start(bf16[3,1,128,64]{2,3,1,0:T(8,128)(2,1)} %param.32) | copy-start | bytes 147460
  27.2 5.2 %copy-start.12 = (pred[16,64]{1,0:T(8,128)(4,1)}, pred[16,64]{1,0:T(8,128)(4,1)S(1)}, u32[]{:S(2)}) copy-start(pred[16,64]{1,0:T(8,128)(4,1)S(1)} %get-tuple-element.25) | copy-start | bytes 3076
  27.5 0.6 copy-start.8
  32.2 1.5 copy-start.2
  43.4 70.4 %all-to-all-start = ((bf16[136,16,640]{2,0,1:T(8,128)(2,1)}), bf16[136,16,640]{2,0,1:T(8,128)(2,1)}, u32[]{:S(2)}, u32[]{:S(2)}) async-start(bf16[136,16,640]{2,0,1:T(8,128)(2,1)} %copy.71), calls=%async_computation | async-start | bytes 5570560 | tf_op jit(solution)/shard_map/all_to_all | solution.py:72
  50.7 71.0 %all-gather.5.cloned.1.call-start = ((), (), s32[]{:S(2)}) async-start(), calls=%async_computation.5 | async-start | bytes 2228224 | tf_op jit(solution)/shard_map/all_gather | solution.py:117
  124.6 1.3 copy-start.3
  126.9 2.8 collective-permute-start
  134.8 33.3 %all-to-all-start.2 = ((f32[8,64,448]{2,1,0:T(8,128)}), f32[8,64,448]{2,1,0:T(8,128)}, u32[]{:S(2)}, u32[]{:S(2)}) async-start(f32[8,64,448]{2,1,0:T(8,128)} %bitcast.116), calls=%async_computation.2 | async-start | bytes 2097152 | tf_op jit(solution)/shard_map/all_to_all | solution.py:132
  140.4 118.4 %all-gather.7.cloned.1.call-start = ((), (), s32[]{:S(2)}) async-start(), calls=%async_computation.6 | async-start | bytes 9748480 | tf_op jit(solution)/shard_map/all_gather | solution.py:145
  171.0 0.6 copy-start.5
  197.3 0.8 copy-start.7
  205.6 104.0 %all-gather.9.cloned.1.call-start = ((), (), s32[]{:S(2)}) async-start(), calls=%async_computation.7 | async-start | bytes 2785280 | tf_op jit(solution)/shard_map/all_gather | solution.py:150
  258.8 6.8 %copy-start.19 = (bf16[640,7168]{1,0:T(8,128)(2,1)S(1)}, bf16[640,7168]{1,0:T(8,128)(2,1)}, u32[]{:S(2)}) copy-start(bf16[640,7168]{1,0:T(8,128)(2,1)} %all-gather.7.cloned.1.call-done) | copy-start | bytes 27525124
  258.8 7.2 %copy-start.20 = (bf16[1,7168,128]{2,1,0:T(8,128)(2,1)S(1)}, bf16[1,7168,128]{2,1,0:T(8,128)(2,1)}, u32[]{:S(2)}) copy-start(bf16[1,7168,128]{2,1,0:T(8,128)(2,1)} %param.30) | copy-start | bytes 5505028
  266.0 3.2 copy-start.14
  314.0 2.7 copy-start.1
  316.7 3.3 copy-start.10
  321.7 32.7 %copy-start.16 = (s32[64,8]{0,1:T(8,128)S(1)}, s32[64,8]{0,1:T(8,128)}, u32[]{:S(2)}) copy-start(s32[64,8]{0,1:T(8,128)} %param.26) | copy-start | bytes 6148
  321.7 32.7 %copy-start.17 = (f32[64,8]{0,1:T(8,128)S(1)}, f32[64,8]{0,1:T(8,128)}, u32[]{:S(2)}) copy-start(f32[64,8]{0,1:T(8,128)} %param.27) | copy-start | bytes 6148
  321.7 44.9 %copy-start.6 = (bf16[64,448]{1,0:T(8,128)(2,1)S(1)}, bf16[64,448]{1,0:T(8,128)(2,1)}, u32[]{:S(2)}) copy-start(bf16[64,448]{1,0:T(8,128)(2,1)} %copy-done.5) | copy-start | bytes 172036
  321.7 44.9 %copy-start.13 = (pred[16,64]{1,0:T(8,128)(4,1)S(1)}, pred[16,64]{1,0:T(8,128)(4,1)}, u32[]{:S(2)}) copy-start(pred[16,64]{1,0:T(8,128)(4,1)} %copy-done.12) | copy-start | bytes 3076
  347.6 19.0 %all-to-all-start.4 = ((bf16[16,40,448]{2,1,0:T(8,128)(2,1)}), bf16[16,40,448]{2,1,0:T(8,128)(2,1)S(1)}, u32[]{:S(2)}, u32[]{:S(2)}) async-start(bf16[16,40,448]{2,1,0:T(8,128)(2,1)} %all_to_all.48), calls=%async_computation.4 | async-start | bytes 1310720 | tf_op jit(solution)/shard_map/all_to_all | solution.py:163
Sparse Core Ops, SparseCore 0:
  53.9 51.1 all-gather.4
  205.7 53.0 all-gather.6
  269.4 40.1 all-gather.8

commit v2 on v1

--- a/solution.py
+++ b/solution.py
@@ -59,17 +59,18 @@
     mine_owner = jnp.sum(mine.astype(jnp.int32) * tenant_ids[None, :], axis=1)
     hidden_slice = expert_down_weight.shape[1]
     down_local = expert_down_weight[0].reshape(hidden_slice, n_slices, col_width)
+    down_local = jnp.transpose(down_local, (1, 0, 2))
     left_local = left_delta_factor[:, 0]
     tenants, _, rank = left_local.shape
-    left_local = jnp.transpose(left_local, (1, 0, 2)).reshape(hidden_slice, 1, tenants * rank)
-    left_local = jnp.broadcast_to(left_local, (hidden_slice, n_slices, tenants * rank))
+    left_local = jnp.transpose(left_local, (1, 0, 2)).reshape(1, hidden_slice, tenants * rank)
+    left_local = jnp.broadcast_to(left_local, (n_slices, hidden_slice, tenants * rank))
     down_pack = jnp.concatenate([down_local, left_local], axis=2)
     pack_width = down_pack.shape[2]
     info = mine_owner.astype(jnp.bfloat16)
     info_rows = jnp.zeros((8, pack_width), jnp.bfloat16).at[0, : info.shape[0]].set(info)
-    info_rows = jnp.broadcast_to(info_rows[:, None, :], (8, n_slices, pack_width))
-    down_pack = jnp.concatenate([down_pack, info_rows], axis=0)
-    down_pack = lax.all_to_all(down_pack, RT, split_axis=1, concat_axis=0, tiled=True)
+    info_rows = jnp.broadcast_to(info_rows[None], (n_slices, 8, pack_width))
+    down_pack = jnp.concatenate([down_pack, info_rows], axis=1)
+    down_pack = lax.all_to_all(down_pack, RT, split_axis=0, concat_axis=0, tiled=True)
     right_w = lax.dynamic_slice_in_dim(factor_right[:, 0], slice_idx * col_width, col_width, 2)
 
     seq_count, context, width = latent_cache.shape
@@ -115,7 +116,6 @@
         head_values.shape[0], head_values.shape[1] * head_values.shape[2]
     )
     all_values = lax.all_gather(head_values, "dp", axis=0, tiled=True)
-    down_pack = down_pack.reshape(n_slices, hidden_slice + 8, pack_width)
     owners = down_pack[:, hidden_slice, :capacity].astype(jnp.int32).reshape(n_slices * capacity)
     down_pack = down_pack[:, :hidden_slice].reshape(n_slices * hidden_slice, pack_width)
     down_w = down_pack[:, :col_width]
@@ -129,8 +129,8 @@
     partial = keep + lax.ppermute(give, "role", [(0, 1), (1, 0)])
     n_tensor = lax.axis_size("tensor")
     partial = partial.reshape(n_tensor, partial.shape[0] // n_tensor, partial.shape[1])
-    partial = lax.all_to_all(partial, "tensor", split_axis=0, concat_axis=0, tiled=True)
-    attention = jnp.sum(partial, axis=0)
+    partial = lax.all_to_all(partial.astype(jnp.bfloat16), "tensor", split_axis=0, concat_axis=0, tiled=True)
+    attention = jnp.sum(partial.astype(jnp.float32), axis=0)
     mixed_in = lax.optimization_barrier(
         (residual.astype(jnp.float32) + attention).astype(jnp.bfloat16)
     )

time: 376 us -> 363 us (0.965)
  waiting for transfers between devices: 195 us -> 183 us
    all_to_all x2, waiting for transfers between devices: 87.1 us -> 75.9 us  [the longest x1 60.8 us: local(): lax.all_to_all(down_pack, RT, split_axis=0, concat_axis=0, tiled=True)]
where the time goes in v2:
time: 363 us; the launch traced here: 361 us
  waiting for transfers between devices  183 us (50%)
  blocking collectives  50.2 us (14%)
  local copies, waits for them, and re-layouts  37.5 us (10%)
  matrix products  33.9 us (9%)
  starting transfers between devices  28.7 us (8%)
  other arithmetic  14.2 us (4%)
  between operations  13.5 us (4%)
    all_to_all x1, waiting for transfers between devices, local(): lax.all_to_all(down_pack, RT, split_axis=0, concat_axis=0, tiled=True)  60.8 us
    all_gather x1, waiting for transfers between devices, local(): collected_rows = lax.all_gather(picked, RT, axis=0, tiled=True)  53.2 us
    all_gather x1, waiting for transfers between devices, local(): gathered = lax.all_gather(hidden, RT, axis=0, tiled=False)  39.7 us
    all_gather x1, blocking collectives, local(): full_rows = lax.all_gather(mixed_in, 'dp', axis=0, tiled=True)  25.7 us
    all_to_all x1, blocking collectives, local(): lax.all_to_all(expert_out, RT, split_axis=0, concat_axis=0, tiled=True)  24.6 us
    all_to_all x1, waiting for transfers between devices, local(): lax.all_to_all(partial.astype(jnp.bfloat16), 'tensor', split_axis=0, conc...  15 us
    all_to_all x1, waiting for transfers between devices, local(): lax.all_to_all(by_group, 'dp', split_axis=0, concat_axis=0, tiled=True)  12.1 us
    all_to_all x1, starting transfers between devices, local(): lax.all_to_all(attended, 'tensor', split_axis=1, concat_axis=0, tiled=True)  8.57 us
  transfers between devices with their start and end apart: 8, of which 6 were waited for; matrix products, arithmetic and copies ran while one was open for 7% of the time, Pallas kernels for 0%

profile of v2, /device:TPU:32, one launch (start us, length us, event | category | flops | bytes accessed | tf_op | source)
XLA Modules:
  0.0 361.4 jit_solution(1481448943356265534)
XLA Ops:
  6.5 0.9 iota_compare_fusion.3
  7.4 0.7 reshape.193
  8.2 3.9 %fusion.7 = (f32[4,2,64]{2,1,0:T(2,128)S(1)}, f32[4,2,64,1024]{3,2,1,0:T(8,128)S(1)}) fusion(pred[4,1024]{1,0:T(4,128)(4,1)S(1)} %iota_compare_fusion.3, bf16[4,2,64,576]{3,2,1,0:T(8,128)(2,1)} %bitcast.118, bf16[4,1024,576]{1,2,0:T(8,128)(2,1)} %param.19), kind=kOutput, calls=%fused_computation.13 | convolution fusion | flops 605552128 | bytes 7411712 | tf_op jit(solution)/shard_map/sqhd,spd->sqhp/dot_general | solution.py:80
  12.1 0.4 fusion.60
  12.6 0.6 fusion.12
  13.2 2.5 fusion.2
  15.8 1.6 fusion.17
  17.4 1.1 copy.74
  18.5 8.6 %all-to-all-start.1 = ((bf16[8,64,512]{2,0,1:T(8,128)(2,1)}), bf16[8,64,512]{2,0,1:T(8,128)(2,1)S(1)}, u32[]{:S(2)}, u32[]{:S(2)}) async-start(bf16[8,64,512]{2,0,1:T(8,128)(2,1)} %copy.74), calls=%async_computation.1 | async-start | bytes 1048576 | tf_op jit(solution)/shard_map/all_to_all | solution.py:111
  27.2 0.2 reduce_window_sum.11
  27.4 0.1 fusion.38
  27.5 0.6 copy-done.8
  28.1 0.1 select_reduce_fusion.1
  28.2 0.1 copy.88
  28.3 3.9 %copy.69 = bf16[1,128,7168]{1,2,0:T(8,128)(2,1)} copy(bf16[1,128,7168]{2,1,0:T(8,128)(2,1)} %param.31) | data formatting | bytes 3670016 | tf_op args[13]
  32.3 0.5 broadcast_in_dim.28
  32.8 0.9 copy-done.2
  33.7 3.5 pad_maximum_fusion
  37.2 6.2 %copy.71 = bf16[16,136,640]{2,1,0:T(8,128)(2,1)} copy(bf16[16,136,640]{1,2,0:T(8,128)(2,1)} %pad_maximum_fusion) | data formatting | bytes 5570560 | tf_op jit(solution)/shard_map/concatenate | solution.py:72
  43.4 7.2 %all-to-all-start = ((bf16[16,136,640]{2,1,0:T(8,128)(2,1)}), bf16[16,136,640]{2,1,0:T(8,128)(2,1)}, u32[]{:S(2)}, u32[]{:S(2)}) async-start(bf16[16,136,640]{2,1,0:T(8,128)(2,1)} %copy.71), calls=%async_computation | async-start | bytes 5570560 | tf_op jit(solution)/shard_map/all_to_all | solution.py:73
  50.7 1.5 fusion.25
  52.3 0.7 copy.102
  53.0 60.8 %all-to-all-done = bf16[16,136,640]{2,1,0:T(8,128)(2,1)} async-done(((bf16[16,136,640]{2,1,0:T(8,128)(2,1)}), bf16[16,136,640]{2,1,0:T(8,128)(2,1)}, u32[]{:S(2)}, u32[]{:S(2)}) %all-to-all-start) | async-done | bytes 2785312 | tf_op jit(solution)/shard_map/all_to_all | solution.py:73
  113.8 2.0 slice.40
  115.8 1.5 slice.41
  117.3 1.4 slice.42
  118.7 1.4 copy.72
  120.1 0.8 fusion.49
  120.9 0.7 reshape.188
  121.6 3.0 fusion.61
  124.6 1.3 copy-done.3
  125.8 1.0 constant_dynamic-slice_fusion
  126.9 0.4 collective-permute-start
  127.3 2.4 collective-permute-done
  129.7 2.4 add_convert_fusion
  132.1 2.0 copy.77
  134.1 5.6 %all-to-all-start.2 = ((bf16[8,64,448]{2,1,0:T(8,128)(2,1)}), bf16[8,64,448]{2,1,0:T(8,128)(2,1)}, u32[]{:S(2)}, u32[]{:S(2)}) async-start(bf16[8,64,448]{2,1,0:T(8,128)(2,1)} %bitcast.116), calls=%async_computation.2 | async-start | bytes 1048576 | tf_op jit(solution)/shard_map/all_to_all | solution.py:132
  139.7 1.4 reshape.190
  141.1 15.0 %all-to-all-done.2 = bf16[8,64,448]{2,1,0:T(8,128)(2,1)} async-done(((bf16[8,64,448]{2,1,0:T(8,128)(2,1)}), bf16[8,64,448]{2,1,0:T(8,128)(2,1)}, u32[]{:S(2)}, u32[]{:S(2)}) %all-to-all-start.2) | async-done | bytes 458784 | tf_op jit(solution)/shard_map/all_to_all | solution.py:132
  156.2 1.1 convert_reduce_fusion
  157.3 0.9 add_convert_fusion.1
  158.2 0.6 copy-done.5
  158.8 25.7 %all_gather.16 = bf16[1024,448]{1,0:T(8,128)(2,1)S(1)} all-gather(bf16[64,448]{1,0:T(8,128)(2,1)S(1)} %add_convert_fusion.1), channel_id=1, replica_groups=mesh['role'=2,'dp'=16,'tensor'=8] {'dp'}, dimensions={0}, use_global_device_ids=true | all-gather | bytes 974848 | tf_op jit(solution)/shard_map/all_gather | solution.py:138
  184.5 0.3 bitcast_convert_fusion
  184.8 0.3 multiply_reduce_fusion
  185.1 0.1 copy-done.7
  185.3 2.3 fusion.29
  187.6 2.9 convert_element_type.129
  190.5 2.3 convolution_convert_fusion
  192.9 53.2 %all-gather.7.cloned.1.call-done = bf16[640,7168]{1,0:T(8,128)(2,1)} async-done(((bf16[40,7168]{1,0:T(8,128)(2,1)}), bf16[640,7168]{1,0:T(8,128)(2,1)}) %all-gather.7.cloned.1.call-update) | async-done | bytes 9175056 | tf_op jit(solution)/shard_map/all_gather | solution.py:145
  246.0 6.8 %fusion.10 = f32[640,128]{1,0:T(8,128)S(1)} fusion(bf16[640,7168]{1,0:T(8,128)(2,1)} %all-gather.7.cloned.1.call-done, bf16[1,7168,128]{2,1,0:T(8,128)(2,1)} %param.29), kind=kOutput, calls=%fused_computation.16 | convolution fusion | flops 1174405120 | bytes 11337728 | tf_op jit(solution)/shard_map/dot_general | solution.py:146
  252.8 0.4 copy-done.20
  253.3 3.2 fusion.21
  256.5 0.6 fusion.48
  257.1 39.7 %all-gather.9.cloned.1.call-done = bf16[10240,128]{1,0:T(8,128)(2,1)} async-done(((bf16[640,128]{1,0:T(8,128)(2,1)}), bf16[10240,128]{1,0:T(8,128)(2,1)}) %all-gather.9.cloned.1.call-update) | async-done | bytes 2621456 | tf_op jit(solution)/shard_map/all_gather | solution.py:150
  296.8 4.4 %copy.79 = bf16[16,640,128]{1,2,0:T(8,128)(2,1)} copy(bf16[16,640,128]{2,1,0:T(8,128)(2,1)} %bitcast.113) | data formatting | bytes 5242880 | tf_op jit(solution)/shard_map/all_gather | solution.py:150
  301.2 2.7 fusion.63
  303.9 3.3 fusion.62
  307.2 1.7 fusion.16
  308.9 1.3 copy.81
  310.2 24.6 %all_to_all.38 = bf16[16,40,448]{2,1,0:T(8,128)(2,1)} all-to-all(bf16[16,40,448]{2,1,0:T(8,128)(2,1)S(1)} %bitcast.114), channel_id=1, replica_groups=mesh['role'=2,'dp'=16,'tensor'=8] {'role','tensor'}, dimensions={0} | all-to-all | bytes 1146880 | tf_op jit(solution)/shard_map/all_to_all | solution.py:162
  334.8 6.8 %all-to-all-start.4 = ((bf16[16,40,448]{2,1,0:T(8,128)(2,1)}), bf16[16,40,448]{2,1,0:T(8,128)(2,1)S(1)}, u32[]{:S(2)}, u32[]{:S(2)}) async-start(bf16[16,40,448]{2,1,0:T(8,128)(2,1)} %all_to_all.38), calls=%async_computation.4 | async-start | bytes 1310720 | tf_op jit(solution)/shard_map/all_to_all | solution.py:163
  341.6 12.1 %all-to-all-done.4 = bf16[16,40,448]{2,1,0:T(8,128)(2,1)S(1)} async-done(((bf16[16,40,448]{2,1,0:T(8,128)(2,1)}), bf16[16,40,448]{2,1,0:T(8,128)(2,1)S(1)}, u32[]{:S(2)}, u32[]{:S(2)}) %all-to-all-start.4) | async-done | bytes 573472 | tf_op jit(solution)/shard_map/all_to_all | solution.py:163
  353.8 1.1 fusion.26
  (62 shorter events, 0.4 us)
Async XLA Ops:
  6.5 300.6 %copy-start = (bf16[3,1,64,7168]{3,2,1,0:T(8,128)(2,1)S(1)}, bf16[3,1,64,7168]{3,2,1,0:T(8,128)(2,1)}, u32[]{:S(2)}) copy-start(bf16[3,1,64,7168]{3,2,1,0:T(8,128)(2,1)} %param.33) | copy-start | bytes 8257540
  8.1 5.0 %slice-start = ((s8[4718592]{0:T(1024)(128)(4,1)}), s8[4194304]{0:T(1024)(128)(4,1)S(1)}, s32[]{:S(2)}) async-start(s8[4718592]{0:T(1024)(128)(4,1)} %bitcast.111), calls=%async_computation.8 | async-start | bytes 8388608
  8.1 4.0 %copy-start.4 = (bf16[8,64,576]{2,1,0:T(8,128)(2,1)S(1)}, bf16[8,64,576]{2,1,0:T(8,128)(2,1)}, u32[]{:S(2)}) copy-start(bf16[8,64,576]{2,1,0:T(8,128)(2,1)} %param.18) | copy-start | bytes 1769476
  8.2 5.0 %slice-start.1 = ((s8[4718592]{0:T(1024)(128)(4,1)}), s8[524288]{0:T(1024)(128)(4,1)S(1)}, s32[]{:S(2)}) async-start(s8[4718592]{0:T(1024)(128)(4,1)} %bitcast.111), calls=%async_computation.9 | async-start | bytes 1048576
  13.2 2.5 copy-start.11
  15.8 11.3 %copy-start.15 = (s32[64,8]{0,1:T(8,128)S(1)}, s32[64,8]{0,1:T(8,128)}, u32[]{:S(2)}) copy-start(s32[64,8]{0,1:T(8,128)} %param.26) | copy-start | bytes 6148
  17.4 10.7 %copy-start.18 = (s32[64]{0:T(128)S(1)}, s32[64]{0:T(128)}, u32[]{:S(2)}) copy-start(s32[64]{0:T(128)} %param.28) | copy-start | bytes 772
  18.5 24.9 %all-to-all-start.1 = ((bf16[8,64,512]{2,0,1:T(8,128)(2,1)}), bf16[8,64,512]{2,0,1:T(8,128)(2,1)S(1)}, u32[]{:S(2)}, u32[]{:S(2)}) async-start(bf16[8,64,512]{2,0,1:T(8,128)(2,1)} %copy.74), calls=%async_computation.1 | async-start | bytes 1048576 | tf_op jit(solution)/shard_map/all_to_all | solution.py:111
  27.1 5.2 %copy-start.9 = (bf16[3,1,128,64]{2,3,1,0:T(8,128)(2,1)S(1)}, bf16[3,1,128,64]{2,3,1,0:T(8,128)(2,1)}, u32[]{:S(2)}) copy-start(bf16[3,1,128,64]{2,3,1,0:T(8,128)(2,1)} %param.32) | copy-start | bytes 147460
  27.2 5.2 %copy-start.12 = (pred[16,64]{1,0:T(8,128)(4,1)}, pred[16,64]{1,0:T(8,128)(4,1)S(1)}, u32[]{:S(2)}) copy-start(pred[16,64]{1,0:T(8,128)(4,1)S(1)} %get-tuple-element.25) | copy-start | bytes 3076
  27.5 0.6 copy-start.8
  32.2 1.5 copy-start.2
  43.4 70.4 %all-to-all-start = ((bf16[16,136,640]{2,1,0:T(8,128)(2,1)}), bf16[16,136,640]{2,1,0:T(8,128)(2,1)}, u32[]{:S(2)}, u32[]{:S(2)}) async-start(bf16[16,136,640]{2,1,0:T(8,128)(2,1)} %copy.71), calls=%async_computation | async-start | bytes 5570560 | tf_op jit(solution)/shard_map/all_to_all | solution.py:73
  50.7 71.0 %all-gather.5.cloned.1.call-start = ((), (), s32[]{:S(2)}) async-start(), calls=%async_computation.5 | async-start | bytes 2228224 | tf_op jit(solution)/shard_map/all_gather | solution.py:118
  124.6 1.3 copy-start.3
  126.9 2.8 collective-permute-start
  134.1 22.1 %all-to-all-start.2 = ((bf16[8,64,448]{2,1,0:T(8,128)(2,1)}), bf16[8,64,448]{2,1,0:T(8,128)(2,1)}, u32[]{:S(2)}, u32[]{:S(2)}) async-start(bf16[8,64,448]{2,1,0:T(8,128)(2,1)} %bitcast.116), calls=%async_computation.2 | async-start | bytes 1048576 | tf_op jit(solution)/shard_map/all_to_all | solution.py:132
  139.7 106.3 %all-gather.7.cloned.1.call-start = ((), (), s32[]{:S(2)}) async-start(), calls=%async_computation.6 | async-start | bytes 9748480 | tf_op jit(solution)/shard_map/all_gather | solution.py:145
  158.2 0.6 copy-start.5
  184.5 0.8 copy-start.7
  192.8 104.0 %all-gather.9.cloned.1.call-start = ((), (), s32[]{:S(2)}) async-start(), calls=%async_computation.7 | async-start | bytes 2785280 | tf_op jit(solution)/shard_map/all_gather | solution.py:150
  246.0 6.8 %copy-start.19 = (bf16[640,7168]{1,0:T(8,128)(2,1)S(1)}, bf16[640,7168]{1,0:T(8,128)(2,1)}, u32[]{:S(2)}) copy-start(bf16[640,7168]{1,0:T(8,128)(2,1)} %all-gather.7.cloned.1.call-done) | copy-start | bytes 27525124
  246.0 7.2 %copy-start.20 = (bf16[1,7168,128]{2,1,0:T(8,128)(2,1)S(1)}, bf16[1,7168,128]{2,1,0:T(8,128)(2,1)}, u32[]{:S(2)}) copy-start(bf16[1,7168,128]{2,1,0:T(8,128)(2,1)} %param.30) | copy-start | bytes 5505028
  253.3 3.2 copy-start.14
  301.2 2.7 copy-start.1
  303.9 3.3 copy-start.10
  308.9 32.7 %copy-start.16 = (s32[64,8]{0,1:T(8,128)S(1)}, s32[64,8]{0,1:T(8,128)}, u32[]{:S(2)}) copy-start(s32[64,8]{0,1:T(8,128)} %param.26) | copy-start | bytes 6148
  308.9 32.7 %copy-start.17 = (f32[64,8]{0,1:T(8,128)S(1)}, f32[64,8]{0,1:T(8,128)}, u32[]{:S(2)}) copy-start(f32[64,8]{0,1:T(8,128)} %param.27) | copy-start | bytes 6148
  308.9 44.9 %copy-start.6 = (bf16[64,448]{1,0:T(8,128)(2,1)S(1)}, bf16[64,448]{1,0:T(8,128)(2,1)}, u32[]{:S(2)}) copy-start(bf16[64,448]{1,0:T(8,128)(2,1)} %copy-done.5) | copy-start | bytes 172036
  308.9 44.9 %copy-start.13 = (pred[16,64]{1,0:T(8,128)(4,1)S(1)}, pred[16,64]{1,0:T(8,128)(4,1)}, u32[]{:S(2)}) copy-start(pred[16,64]{1,0:T(8,128)(4,1)} %copy-done.12) | copy-start | bytes 3076
  334.8 19.0 %all-to-all-start.4 = ((bf16[16,40,448]{2,1,0:T(8,128)(2,1)}), bf16[16,40,448]{2,1,0:T(8,128)(2,1)S(1)}, u32[]{:S(2)}, u32[]{:S(2)}) async-start(bf16[16,40,448]{2,1,0:T(8,128)(2,1)} %all_to_all.38), calls=%async_computation.4 | async-start | bytes 1310720 | tf_op jit(solution)/shard_map/all_to_all | solution.py:163
Sparse Core Ops, SparseCore 0:
  53.9 51.1 all-gather.4
  193.0 53.0 all-gather.6
  256.6 40.1 all-gather.8

commit v3 on v2

--- a/solution.py
+++ b/solution.py
@@ -135,7 +135,9 @@
         (residual.astype(jnp.float32) + attention).astype(jnp.bfloat16)
     )
 
-    full_rows = lax.all_gather(mixed_in, "dp", axis=0, tiled=True)
+    n_dp = lax.axis_size("dp")
+    spread = jnp.broadcast_to(mixed_in[None], (n_dp,) + mixed_in.shape)
+    full_rows = lax.all_to_all(spread, "dp", split_axis=0, concat_axis=0, tiled=True)
     full_rows = full_rows.reshape(-1, group_rows, mixed_in.shape[1])
     full_rows = jnp.transpose(full_rows, (1, 0, 2)).reshape(group_rows, model_width)
     normed = rms_rows(full_rows, norm_gain)

time: 363 us -> 361 us (level)
  blocking collectives: 50.2 us -> 46.5 us
    all_gather x1 -> x0, blocking collectives: 25.7 us -> none  [local(): full_rows = lax.all_gather(mixed_in, 'dp', axis=0, tiled=True)]
    all_to_all x0 -> x1, blocking collectives: none -> 22 us  [local(): lax.all_to_all(partial.astype(jnp.bfloat16), 'tensor', split_axis=0, conc...]
    unnamed x48 -> x46, local copies, waits for them, and re-layouts: 8.09 us -> 7.92 us
where the time goes in v3:
time: 361 us; the launch traced here: 359 us
  waiting for transfers between devices  182 us (50%)
  blocking collectives  46.5 us (13%)
  local copies, waits for them, and re-layouts  40 us (11%)
  matrix products  33.9 us (9%)
  starting transfers between devices  30.4 us (8%)
  between operations  13.5 us (4%)
  other arithmetic  13.3 us (4%)
    all_to_all x1, waiting for transfers between devices, local(): lax.all_to_all(down_pack, RT, split_axis=0, concat_axis=0, tiled=True)  60.8 us
    all_gather x1, waiting for transfers between devices, local(): collected_rows = lax.all_gather(picked, RT, axis=0, tiled=True)  53.2 us
    all_gather x1, waiting for transfers between devices, local(): gathered = lax.all_gather(hidden, RT, axis=0, tiled=False)  39.7 us
    all_to_all x1, blocking collectives, local(): lax.all_to_all(expert_out, RT, split_axis=0, concat_axis=0, tiled=True)  24.6 us
    all_to_all x1, blocking collectives, local(): lax.all_to_all(partial.astype(jnp.bfloat16), 'tensor', split_axis=0, conc...  22 us
    all_to_all x1, waiting for transfers between devices, local(): lax.all_to_all(spread, 'dp', split_axis=0, concat_axis=0, tiled=True)  13.5 us
    all_to_all x1, waiting for transfers between devices, local(): lax.all_to_all(by_group, 'dp', split_axis=0, concat_axis=0, tiled=True)  12.1 us
    all_to_all x1, starting transfers between devices, local(): lax.all_to_all(attended, 'tensor', split_axis=1, concat_axis=0, tiled=True)  8.57 us
  transfers between devices with their start and end apart: 8, of which 6 were waited for; matrix products, arithmetic and copies ran while one was open for 7% of the time, Pallas kernels for 0%

profile of v3, /device:TPU:32, one launch (start us, length us, event | category | flops | bytes accessed | tf_op | source)
XLA Modules:
  0.0 359.5 jit_solution(16311324268286633759)
XLA Ops:
  6.5 0.9 iota_compare_fusion.3
  7.4 0.7 reshape.190
  8.2 3.9 %fusion.8 = (f32[4,2,64]{2,1,0:T(2,128)S(1)}, f32[4,2,64,1024]{3,2,1,0:T(8,128)S(1)}) fusion(pred[4,1024]{1,0:T(4,128)(4,1)S(1)} %iota_compare_fusion.3, bf16[4,2,64,576]{3,2,1,0:T(8,128)(2,1)} %bitcast.114, bf16[4,1024,576]{1,2,0:T(8,128)(2,1)} %param.19), kind=kOutput, calls=%fused_computation.14 | convolution fusion | flops 605552128 | bytes 7411712 | tf_op jit(solution)/shard_map/sqhd,spd->sqhp/dot_general | solution.py:80
  12.1 0.4 fusion.61
  12.6 0.6 fusion.13
  13.2 2.5 fusion.2
  15.8 1.6 fusion.18
  17.4 1.1 copy.72
  18.5 8.6 %all-to-all-start.1 = ((bf16[8,64,512]{2,0,1:T(8,128)(2,1)}), bf16[8,64,512]{2,0,1:T(8,128)(2,1)S(1)}, u32[]{:S(2)}, u32[]{:S(2)}) async-start(bf16[8,64,512]{2,0,1:T(8,128)(2,1)} %copy.72), calls=%async_computation.1 | async-start | bytes 1048576 | tf_op jit(solution)/shard_map/all_to_all | solution.py:111
  27.2 0.2 reduce_window_sum.11
  27.5 0.6 copy-done.7
  28.1 0.1 select_reduce_fusion.1
  28.2 0.1 copy.86
  28.3 3.9 %copy.67 = bf16[1,128,7168]{1,2,0:T(8,128)(2,1)} copy(bf16[1,128,7168]{2,1,0:T(8,128)(2,1)} %param.31) | data formatting | bytes 3670016 | tf_op args[13]
  32.3 0.5 broadcast_in_dim.30
  32.8 0.9 copy-done.2
  33.7 3.5 pad_maximum_fusion
  37.2 6.2 %copy.69 = bf16[16,136,640]{2,1,0:T(8,128)(2,1)} copy(bf16[16,136,640]{1,2,0:T(8,128)(2,1)} %pad_maximum_fusion) | data formatting | bytes 5570560 | tf_op jit(solution)/shard_map/concatenate | solution.py:72
  43.4 7.2 %all-to-all-start = ((bf16[16,136,640]{2,1,0:T(8,128)(2,1)}), bf16[16,136,640]{2,1,0:T(8,128)(2,1)}, u32[]{:S(2)}, u32[]{:S(2)}) async-start(bf16[16,136,640]{2,1,0:T(8,128)(2,1)} %copy.69), calls=%async_computation | async-start | bytes 5570560 | tf_op jit(solution)/shard_map/all_to_all | solution.py:73
  50.7 1.5 fusion.26
  52.3 0.7 copy.93
  53.0 60.8 %all-to-all-done = bf16[16,136,640]{2,1,0:T(8,128)(2,1)} async-done(((bf16[16,136,640]{2,1,0:T(8,128)(2,1)}), bf16[16,136,640]{2,1,0:T(8,128)(2,1)}, u32[]{:S(2)}, u32[]{:S(2)}) %all-to-all-start) | async-done | bytes 2785312 | tf_op jit(solution)/shard_map/all_to_all | solution.py:73
  113.8 2.0 slice.40
  115.8 1.5 slice.41
  117.3 1.4 slice.42
  118.7 1.4 copy.70
  120.2 0.8 fusion.50
  121.0 0.7 reshape.186
  121.6 3.0 fusion.62
  124.6 1.2 copy-done.3
  125.8 1.0 constant_dynamic-slice_fusion
  126.9 0.4 collective-permute-start
  127.3 2.4 collective-permute-done
  129.7 2.4 add_convert_fusion
  132.1 2.0 copy.75
  134.1 22.0 %all_to_all.43 = bf16[8,64,448]{2,1,0:T(8,128)(2,1)S(1)} all-to-all(bf16[8,64,448]{2,1,0:T(8,128)(2,1)} %bitcast.112), channel_id=1, replica_groups=mesh['role'=2,'dp'=16,'tensor'=8] {'tensor'}, dimensions={0} | all-to-all | bytes 917504 | tf_op jit(solution)/shard_map/all_to_all | solution.py:132
  156.1 0.1 convert_reduce_fusion
  156.2 0.9 add_convert_fusion.1
  157.0 0.6 copy-done.5
  157.7 1.1 broadcast_in_dim.39
  158.8 7.1 %all-to-all-start.3 = ((bf16[16,64,448]{2,1,0:T(8,128)(2,1)}), bf16[16,64,448]{2,1,0:T(8,128)(2,1)}, u32[]{:S(2)}, u32[]{:S(2)}) async-start(bf16[16,64,448]{2,1,0:T(8,128)(2,1)} %broadcast_in_dim.39), calls=%async_computation.3 | async-start | bytes 2097152 | tf_op jit(solution)/shard_map/all_to_all | solution.py:140
  165.8 0.2 all-gather.7.cloned.1.call-start
  166.1 1.4 reshape.187
  167.5 13.5 %all-to-all-done.3 = bf16[16,64,448]{2,1,0:T(8,128)(2,1)} async-done(((bf16[16,64,448]{2,1,0:T(8,128)(2,1)}), bf16[16,64,448]{2,1,0:T(8,128)(2,1)}, u32[]{:S(2)}, u32[]{:S(2)}) %all-to-all-start.3) | async-done | bytes 917536 | tf_op jit(solution)/shard_map/all_to_all | solution.py:140
  180.9 1.6 fusion.5
  182.5 1.6 fusion.30
  184.1 1.6 copy.76
  185.6 2.9 convert_element_type.125
  188.5 2.3 convolution_convert_fusion
  190.9 53.2 %all-gather.7.cloned.1.call-done = bf16[640,7168]{1,0:T(8,128)(2,1)} async-done(((bf16[40,7168]{1,0:T(8,128)(2,1)}), bf16[640,7168]{1,0:T(8,128)(2,1)}) %all-gather.7.cloned.1.call-update) | async-done | bytes 9175056 | tf_op jit(solution)/shard_map/all_gather | solution.py:147
  244.1 6.8 %fusion.11 = f32[640,128]{1,0:T(8,128)S(1)} fusion(bf16[640,7168]{1,0:T(8,128)(2,1)} %all-gather.7.cloned.1.call-done, bf16[1,7168,128]{2,1,0:T(8,128)(2,1)} %param.29), kind=kOutput, calls=%fused_computation.17 | convolution fusion | flops 1174405120 | bytes 11337728 | tf_op jit(solution)/shard_map/dot_general | solution.py:148
  250.9 0.4 copy-done.19
  251.3 3.2 fusion.22
  254.6 0.6 fusion.49
  255.2 39.7 %all-gather.9.cloned.1.call-done = bf16[10240,128]{1,0:T(8,128)(2,1)} async-done(((bf16[640,128]{1,0:T(8,128)(2,1)}), bf16[10240,128]{1,0:T(8,128)(2,1)}) %all-gather.9.cloned.1.call-update) | async-done | bytes 2621456 | tf_op jit(solution)/shard_map/all_gather | solution.py:152
  294.9 4.4 %copy.77 = bf16[16,640,128]{1,2,0:T(8,128)(2,1)} copy(bf16[16,640,128]{2,1,0:T(8,128)(2,1)} %bitcast.109) | data formatting | bytes 5242880 | tf_op jit(solution)/shard_map/all_gather | solution.py:152
  299.3 2.7 fusion.64
  302.0 3.3 fusion.63
  305.3 1.7 fusion.17
  306.9 1.3 copy.79
  308.3 24.6 %all_to_all.44 = bf16[16,40,448]{2,1,0:T(8,128)(2,1)} all-to-all(bf16[16,40,448]{2,1,0:T(8,128)(2,1)S(1)} %bitcast.110), channel_id=1, replica_groups=mesh['role'=2,'dp'=16,'tensor'=8] {'role','tensor'}, dimensions={0} | all-to-all | bytes 1146880 | tf_op jit(solution)/shard_map/all_to_all | solution.py:164
  332.8 6.8 %all-to-all-start.5 = ((bf16[16,40,448]{2,1,0:T(8,128)(2,1)}), bf16[16,40,448]{2,1,0:T(8,128)(2,1)S(1)}, u32[]{:S(2)}, u32[]{:S(2)}) async-start(bf16[16,40,448]{2,1,0:T(8,128)(2,1)} %all_to_all.44), calls=%async_computation.5 | async-start | bytes 1310720 | tf_op jit(solution)/shard_map/all_to_all | solution.py:165
  339.7 12.1 %all-to-all-done.5 = bf16[16,40,448]{2,1,0:T(8,128)(2,1)S(1)} async-done(((bf16[16,40,448]{2,1,0:T(8,128)(2,1)}), bf16[16,40,448]{2,1,0:T(8,128)(2,1)S(1)}, u32[]{:S(2)}, u32[]{:S(2)}) %all-to-all-start.5) | async-done | bytes 573472 | tf_op jit(solution)/shard_map/all_to_all | solution.py:165
  351.8 1.1 fusion.27
  (61 shorter events, 0.5 us)
Async XLA Ops:
  6.5 298.7 %copy-start = (bf16[3,1,64,7168]{3,2,1,0:T(8,128)(2,1)S(1)}, bf16[3,1,64,7168]{3,2,1,0:T(8,128)(2,1)}, u32[]{:S(2)}) copy-start(bf16[3,1,64,7168]{3,2,1,0:T(8,128)(2,1)} %param.33) | copy-start | bytes 8257540
  8.1 5.0 %slice-start = ((s8[4718592]{0:T(1024)(128)(4,1)}), s8[4194304]{0:T(1024)(128)(4,1)S(1)}, s32[]{:S(2)}) async-start(s8[4718592]{0:T(1024)(128)(4,1)} %bitcast.107), calls=%async_computation.9 | async-start | bytes 8388608
  8.1 4.0 %copy-start.4 = (bf16[8,64,576]{2,1,0:T(8,128)(2,1)S(1)}, bf16[8,64,576]{2,1,0:T(8,128)(2,1)}, u32[]{:S(2)}) copy-start(bf16[8,64,576]{2,1,0:T(8,128)(2,1)} %param.18) | copy-start | bytes 1769476
  8.2 5.0 %slice-start.1 = ((s8[4718592]{0:T(1024)(128)(4,1)}), s8[524288]{0:T(1024)(128)(4,1)S(1)}, s32[]{:S(2)}) async-start(s8[4718592]{0:T(1024)(128)(4,1)} %bitcast.107), calls=%async_computation.10 | async-start | bytes 1048576
  13.2 2.5 copy-start.10
  15.8 11.3 %copy-start.14 = (s32[64,8]{0,1:T(8,128)S(1)}, s32[64,8]{0,1:T(8,128)}, u32[]{:S(2)}) copy-start(s32[64,8]{0,1:T(8,128)} %param.26) | copy-start | bytes 6148
  17.4 10.7 %copy-start.17 = (s32[64]{0:T(128)S(1)}, s32[64]{0:T(128)}, u32[]{:S(2)}) copy-start(s32[64]{0:T(128)} %param.28) | copy-start | bytes 772
  18.5 24.9 %all-to-all-start.1 = ((bf16[8,64,512]{2,0,1:T(8,128)(2,1)}), bf16[8,64,512]{2,0,1:T(8,128)(2,1)S(1)}, u32[]{:S(2)}, u32[]{:S(2)}) async-start(bf16[8,64,512]{2,0,1:T(8,128)(2,1)} %copy.72), calls=%async_computation.1 | async-start | bytes 1048576 | tf_op jit(solution)/shard_map/all_to_all | solution.py:111
  27.1 5.1 %copy-start.8 = (bf16[3,1,128,64]{2,3,1,0:T(8,128)(2,1)S(1)}, bf16[3,1,128,64]{2,3,1,0:T(8,128)(2,1)}, u32[]{:S(2)}) copy-start(bf16[3,1,128,64]{2,3,1,0:T(8,128)(2,1)} %param.32) | copy-start | bytes 147460
  27.2 5.1 %copy-start.11 = (pred[16,64]{1,0:T(8,128)(4,1)}, pred[16,64]{1,0:T(8,128)(4,1)S(1)}, u32[]{:S(2)}) copy-start(pred[16,64]{1,0:T(8,128)(4,1)S(1)} %get-tuple-element.25) | copy-start | bytes 3076
  27.5 0.6 copy-start.7
  32.2 1.5 copy-start.2
  43.4 70.4 %all-to-all-start = ((bf16[16,136,640]{2,1,0:T(8,128)(2,1)}), bf16[16,136,640]{2,1,0:T(8,128)(2,1)}, u32[]{:S(2)}, u32[]{:S(2)}) async-start(bf16[16,136,640]{2,1,0:T(8,128)(2,1)} %copy.69), calls=%async_computation | async-start | bytes 5570560 | tf_op jit(solution)/shard_map/all_to_all | solution.py:73
  50.7 71.0 %all-gather.5.cloned.1.call-start = ((), (), s32[]{:S(2)}) async-start(), calls=%async_computation.6 | async-start | bytes 2228224 | tf_op jit(solution)/shard_map/all_gather | solution.py:118
  124.6 1.3 copy-start.3
  126.9 2.8 collective-permute-start
  157.0 0.6 copy-start.5
  158.8 22.2 %all-to-all-start.3 = ((bf16[16,64,448]{2,1,0:T(8,128)(2,1)}), bf16[16,64,448]{2,1,0:T(8,128)(2,1)}, u32[]{:S(2)}, u32[]{:S(2)}) async-start(bf16[16,64,448]{2,1,0:T(8,128)(2,1)} %broadcast_in_dim.39), calls=%async_computation.3 | async-start | bytes 2097152 | tf_op jit(solution)/shard_map/all_to_all | solution.py:140
  165.8 78.2 %all-gather.7.cloned.1.call-start = ((), (), s32[]{:S(2)}) async-start(), calls=%async_computation.7 | async-start | bytes 9748480 | tf_op jit(solution)/shard_map/all_gather | solution.py:147
  190.9 104.0 %all-gather.9.cloned.1.call-start = ((), (), s32[]{:S(2)}) async-start(), calls=%async_computation.8 | async-start | bytes 2785280 | tf_op jit(solution)/shard_map/all_gather | solution.py:152
  244.1 6.8 %copy-start.18 = (bf16[640,7168]{1,0:T(8,128)(2,1)S(1)}, bf16[640,7168]{1,0:T(8,128)(2,1)}, u32[]{:S(2)}) copy-start(bf16[640,7168]{1,0:T(8,128)(2,1)} %all-gather.7.cloned.1.call-done) | copy-start | bytes 27525124
  244.1 7.2 %copy-start.19 = (bf16[1,7168,128]{2,1,0:T(8,128)(2,1)S(1)}, bf16[1,7168,128]{2,1,0:T(8,128)(2,1)}, u32[]{:S(2)}) copy-start(bf16[1,7168,128]{2,1,0:T(8,128)(2,1)} %param.30) | copy-start | bytes 5505028
  251.3 3.2 copy-start.13
  299.3 2.7 copy-start.1
  302.0 3.3 copy-start.9
  306.9 32.7 %copy-start.15 = (s32[64,8]{0,1:T(8,128)S(1)}, s32[64,8]{0,1:T(8,128)}, u32[]{:S(2)}) copy-start(s32[64,8]{0,1:T(8,128)} %param.26) | copy-start | bytes 6148
  306.9 32.7 %copy-start.16 = (f32[64,8]{0,1:T(8,128)S(1)}, f32[64,8]{0,1:T(8,128)}, u32[]{:S(2)}) copy-start(f32[64,8]{0,1:T(8,128)} %param.27) | copy-start | bytes 6148
  306.9 44.9 %copy-start.6 = (bf16[64,448]{1,0:T(8,128)(2,1)S(1)}, bf16[64,448]{1,0:T(8,128)(2,1)}, u32[]{:S(2)}) copy-start(bf16[64,448]{1,0:T(8,128)(2,1)} %copy-done.5) | copy-start | bytes 172036
  306.9 44.9 %copy-start.12 = (pred[16,64]{1,0:T(8,128)(4,1)S(1)}, pred[16,64]{1,0:T(8,128)(4,1)}, u32[]{:S(2)}) copy-start(pred[16,64]{1,0:T(8,128)(4,1)} %copy-done.11) | copy-start | bytes 3076
  332.8 19.0 %all-to-all-start.5 = ((bf16[16,40,448]{2,1,0:T(8,128)(2,1)}), bf16[16,40,448]{2,1,0:T(8,128)(2,1)S(1)}, u32[]{:S(2)}, u32[]{:S(2)}) async-start(bf16[16,40,448]{2,1,0:T(8,128)(2,1)} %all_to_all.44), calls=%async_computation.5 | async-start | bytes 1310720 | tf_op jit(solution)/shard_map/all_to_all | solution.py:165
Sparse Core Ops, SparseCore 0:
  53.9 51.1 all-gather.4
  191.0 53.0 all-gather.6
  254.7 40.1 all-gather.8

commit v4 on v3

--- a/solution.py
+++ b/solution.py
@@ -150,11 +150,12 @@
     hidden = (jax.nn.silu(gate_scores) * upper_bound).astype(jnp.bfloat16)
 
     gathered = lax.all_gather(hidden, RT, axis=0, tiled=False)
-    hidden_all = jnp.transpose(gathered, (1, 0, 2)).reshape(hidden.shape[0], -1)
-    base_output = jnp.dot(hidden_all, down_w, preferred_element_type=jnp.float32)
+    down_w = down_w.reshape(n_slices, hidden_slice, col_width)
+    left_w = left_w.reshape(n_slices, hidden_slice, tenants, rank)
+    base_output = jnp.einsum("jsh,jhc->sc", gathered, down_w, preferred_element_type=jnp.float32)
     owner_mask = (owners[:, None] == jnp.arange(TEN, dtype=jnp.int32)[None, :]).astype(jnp.float32)
     mixing = jnp.einsum(
-        "sf,ftr->str", hidden_all, left_w, preferred_element_type=jnp.float32
+        "jsf,jftr->str", gathered, left_w, preferred_element_type=jnp.float32
     ) * owner_mask[:, :, None]
     delta = jnp.einsum(
         "str,trd->sd", mixing, right_w.astype(jnp.float32), precision=lax.Precision.HIGHEST

time: 361 us -> 353 us (0.978)
  local copies, waits for them, and re-layouts: 40 us -> 33.1 us
    all_gather x1 -> x0, local copies, waits for them, and re-layouts: 4.39 us -> none  [local(): gathered = lax.all_gather(hidden, RT, axis=0, tiled=False)]
    unnamed x46 -> x44, local copies, waits for them, and re-layouts: 7.92 us -> 7.32 us
  transfers between devices with their start and end apart: 8 -> 8, of which waited for: 6 -> 7; matrix products, arithmetic and copies ran while one was open for 7% -> 7% of each run, Pallas kernels for 0% -> 0%
where the time goes in v4:
time: 353 us; the launch traced here: 351 us
  waiting for transfers between devices  183 us (52%)
  blocking collectives  46.3 us (13%)
  local copies, waits for them, and re-layouts  33.1 us (9%)
  matrix products  32.5 us (9%)
  starting transfers between devices  30.1 us (9%)
  between operations  13.5 us (4%)
  other arithmetic  12.5 us (4%)
    all_to_all x1, waiting for transfers between devices, local(): lax.all_to_all(down_pack, RT, split_axis=0, concat_axis=0, tiled=True)  60.9 us
    all_gather x1, waiting for transfers between devices, local(): collected_rows = lax.all_gather(picked, RT, axis=0, tiled=True)  53.2 us
    all_gather x1, waiting for transfers between devices, local(): gathered = lax.all_gather(hidden, RT, axis=0, tiled=False)  39.7 us
    all_to_all x1, blocking collectives, local(): lax.all_to_all(expert_out, RT, split_axis=0, concat_axis=0, tiled=True)  24.5 us
    all_to_all x1, blocking collectives, local(): lax.all_to_all(partial.astype(jnp.bfloat16), 'tensor', split_axis=0, conc...  21.8 us
    all_to_all x1, waiting for transfers between devices, local(): lax.all_to_all(spread, 'dp', split_axis=0, concat_axis=0, tiled=True)  14.8 us
    all_to_all x1, waiting for transfers between devices, local(): lax.all_to_all(by_group, 'dp', split_axis=0, concat_axis=0, tiled=True)  12.1 us
    all_to_all x1, starting transfers between devices, local(): lax.all_to_all(attended, 'tensor', split_axis=1, concat_axis=0, tiled=True)  8.57 us
  transfers between devices with their start and end apart: 8, of which 7 were waited for; matrix products, arithmetic and copies ran while one was open for 7% of the time, Pallas kernels for 0%

profile of v4, /device:TPU:32, one launch (start us, length us, event | category | flops | bytes accessed | tf_op | source)
XLA Modules:
  0.0 351.4 jit_solution(2027946078974505955)
XLA Ops:
  6.5 0.9 iota_compare_fusion.3
  7.4 0.7 reshape.194
  8.2 3.9 %fusion.8 = (f32[4,2,64]{2,1,0:T(2,128)S(1)}, f32[4,2,64,1024]{3,2,1,0:T(8,128)S(1)}) fusion(pred[4,1024]{1,0:T(4,128)(4,1)S(1)} %iota_compare_fusion.3, bf16[4,2,64,576]{3,2,1,0:T(8,128)(2,1)} %bitcast.125, bf16[4,1024,576]{1,2,0:T(8,128)(2,1)} %param.19), kind=kOutput, calls=%fused_computation.14 | convolution fusion | flops 605552128 | bytes 7411712 | tf_op jit(solution)/shard_map/sqhd,spd->sqhp/dot_general | solution.py:80
  12.1 0.4 fusion.62
  12.6 0.6 fusion.13
  13.2 2.5 fusion.2
  15.8 1.6 fusion.18
  17.4 1.1 copy.75
  18.5 8.6 %all-to-all-start.1 = ((bf16[8,64,512]{2,0,1:T(8,128)(2,1)}), bf16[8,64,512]{2,0,1:T(8,128)(2,1)S(1)}, u32[]{:S(2)}, u32[]{:S(2)}) async-start(bf16[8,64,512]{2,0,1:T(8,128)(2,1)} %copy.75), calls=%async_computation.1 | async-start | bytes 1048576 | tf_op jit(solution)/shard_map/all_to_all | solution.py:111
  27.2 0.2 reduce_window_sum.11
  27.4 0.1 fusion.41
  27.5 0.1 select_reduce_fusion.1
  27.6 0.1 copy.92
  27.7 3.9 %copy.70 = bf16[1,128,7168]{1,2,0:T(8,128)(2,1)} copy(bf16[1,128,7168]{2,1,0:T(8,128)(2,1)} %param.31) | data formatting | bytes 3670016 | tf_op args[13]
  31.7 0.5 broadcast_in_dim.30
  32.2 0.9 copy-done.1
  33.1 3.5 pad_maximum_fusion
  36.6 6.3 %copy.72 = bf16[16,136,640]{2,1,0:T(8,128)(2,1)} copy(bf16[16,136,640]{1,2,0:T(8,128)(2,1)} %pad_maximum_fusion) | data formatting | bytes 5570560 | tf_op jit(solution)/shard_map/concatenate | solution.py:72
  42.8 0.3 all-to-all-done.1
  43.1 6.9 %all-to-all-start = ((bf16[16,136,640]{2,1,0:T(8,128)(2,1)}), bf16[16,136,640]{2,1,0:T(8,128)(2,1)}, u32[]{:S(2)}, u32[]{:S(2)}) async-start(bf16[16,136,640]{2,1,0:T(8,128)(2,1)} %copy.72), calls=%async_computation | async-start | bytes 5570560 | tf_op jit(solution)/shard_map/all_to_all | solution.py:73
  50.1 1.5 fusion.27
  51.7 0.7 copy.104
  52.4 60.9 %all-to-all-done = bf16[16,136,640]{2,1,0:T(8,128)(2,1)} async-done(((bf16[16,136,640]{2,1,0:T(8,128)(2,1)}), bf16[16,136,640]{2,1,0:T(8,128)(2,1)}, u32[]{:S(2)}, u32[]{:S(2)}) %all-to-all-start) | async-done | bytes 2785312 | tf_op jit(solution)/shard_map/all_to_all | solution.py:73
  113.2 2.0 slice.40
  115.2 1.5 slice.41
  116.7 1.4 slice.42
  118.1 2.2 copy.73
  120.3 0.8 fusion.51
  121.1 0.1 reshape.190
  121.2 3.0 fusion.63
  124.2 1.2 copy-done.3
  125.4 1.0 constant_dynamic-slice_fusion
  126.5 0.4 collective-permute-start
  126.8 2.4 collective-permute-done
  129.3 2.4 add_convert_fusion
  131.7 1.2 copy.78
  132.9 21.8 %all_to_all.43 = bf16[8,64,448]{2,1,0:T(8,128)(2,1)S(1)} all-to-all(bf16[8,64,448]{2,1,0:T(8,128)(2,1)S(1)} %bitcast.123), channel_id=1, replica_groups=mesh['role'=2,'dp'=16,'tensor'=8] {'tensor'}, dimensions={0} | all-to-all | bytes 917504 | tf_op jit(solution)/shard_map/all_to_all | solution.py:132
  154.7 0.1 convert_reduce_fusion
  154.8 0.6 copy-done.6
  155.4 1.1 broadcast_in_dim.39
  156.5 7.1 %all-to-all-start.3 = ((bf16[16,64,448]{2,1,0:T(8,128)(2,1)}), bf16[16,64,448]{2,1,0:T(8,128)(2,1)}, u32[]{:S(2)}, u32[]{:S(2)}) async-start(bf16[16,64,448]{2,1,0:T(8,128)(2,1)} %broadcast_in_dim.39), calls=%async_computation.3 | async-start | bytes 2097152 | tf_op jit(solution)/shard_map/all_to_all | solution.py:140
  163.6 0.2 all-gather.7.cloned.1.call-start
  163.9 0.1 reshape.191
  163.9 14.8 %all-to-all-done.3 = bf16[16,64,448]{2,1,0:T(8,128)(2,1)} async-done(((bf16[16,64,448]{2,1,0:T(8,128)(2,1)}), bf16[16,64,448]{2,1,0:T(8,128)(2,1)}, u32[]{:S(2)}, u32[]{:S(2)}) %all-to-all-start.3) | async-done | bytes 917536 | tf_op jit(solution)/shard_map/all_to_all | solution.py:140
  178.7 1.6 fusion.5
  180.3 1.6 fusion.31
  181.8 1.5 copy.79
  183.4 2.9 convert_element_type.125
  186.3 2.3 convolution_convert_fusion
  188.6 0.0 all-gather.9.cloned.1.call-start
  188.7 53.2 %all-gather.7.cloned.1.call-done = bf16[640,7168]{1,0:T(8,128)(2,1)} async-done(((bf16[40,7168]{1,0:T(8,128)(2,1)}), bf16[640,7168]{1,0:T(8,128)(2,1)}) %all-gather.7.cloned.1.call-update) | async-done | bytes 9175056 | tf_op jit(solution)/shard_map/all_gather | solution.py:147
  241.8 6.8 %fusion.11 = f32[640,128]{1,0:T(8,128)S(1)} fusion(bf16[640,7168]{1,0:T(8,128)(2,1)} %all-gather.7.cloned.1.call-done, bf16[1,7168,128]{2,1,0:T(8,128)(2,1)} %param.29), kind=kOutput, calls=%fused_computation.17 | convolution fusion | flops 1174405120 | bytes 11337728 | tf_op jit(solution)/shard_map/dot_general | solution.py:148
  248.6 0.4 copy-done.18
  249.1 3.2 fusion.23
  252.3 0.6 fusion.50
  252.9 39.7 %all-gather.9.cloned.1.call-done = bf16[10240,128]{1,0:T(8,128)(2,1)} async-done(((bf16[640,128]{1,0:T(8,128)(2,1)}), bf16[10240,128]{1,0:T(8,128)(2,1)}) %all-gather.9.cloned.1.call-update) | async-done | bytes 2621456 | tf_op jit(solution)/shard_map/all_gather | solution.py:152
  292.6 2.9 fusion.19
  295.6 0.8 convolution_bitcast_fusion
  296.4 2.4 fusion.17
  298.9 1.3 copy.83
  300.2 24.5 %all_to_all.44 = bf16[16,40,448]{2,1,0:T(8,128)(2,1)} all-to-all(bf16[16,40,448]{2,1,0:T(8,128)(2,1)S(1)} %bitcast.120), channel_id=1, replica_groups=mesh['role'=2,'dp'=16,'tensor'=8] {'role','tensor'}, dimensions={0} | all-to-all | bytes 1146880 | tf_op jit(solution)/shard_map/all_to_all | solution.py:165
  324.8 6.8 %all-to-all-start.5 = ((bf16[16,40,448]{2,1,0:T(8,128)(2,1)}), bf16[16,40,448]{2,1,0:T(8,128)(2,1)S(1)}, u32[]{:S(2)}, u32[]{:S(2)}) async-start(bf16[16,40,448]{2,1,0:T(8,128)(2,1)} %all_to_all.44), calls=%async_computation.5 | async-start | bytes 1310720 | tf_op jit(solution)/shard_map/all_to_all | solution.py:166
  331.6 12.1 %all-to-all-done.5 = bf16[16,40,448]{2,1,0:T(8,128)(2,1)S(1)} async-done(((bf16[16,40,448]{2,1,0:T(8,128)(2,1)}), bf16[16,40,448]{2,1,0:T(8,128)(2,1)S(1)}, u32[]{:S(2)}, u32[]{:S(2)}) %all-to-all-start.5) | async-done | bytes 573472 | tf_op jit(solution)/shard_map/all_to_all | solution.py:166
  343.8 1.1 fusion.28
  (58 shorter events, 0.4 us)
Async XLA Ops:
  6.5 289.0 %copy-start = (bf16[3,1,64,7168]{3,2,1,0:T(8,128)(2,1)S(1)}, bf16[3,1,64,7168]{3,2,1,0:T(8,128)(2,1)}, u32[]{:S(2)}) copy-start(bf16[3,1,64,7168]{3,2,1,0:T(8,128)(2,1)} %param.33) | copy-start | bytes 8257540
  8.1 5.0 %slice-start = ((s8[4718592]{0:T(1024)(128)(4,1)}), s8[4194304]{0:T(1024)(128)(4,1)S(1)}, s32[]{:S(2)}) async-start(s8[4718592]{0:T(1024)(128)(4,1)} %bitcast.118), calls=%async_computation.9 | async-start | bytes 8388608
  8.1 4.0 %copy-start.5 = (bf16[8,64,576]{2,1,0:T(8,128)(2,1)S(1)}, bf16[8,64,576]{2,1,0:T(8,128)(2,1)}, u32[]{:S(2)}) copy-start(bf16[8,64,576]{2,1,0:T(8,128)(2,1)} %param.18) | copy-start | bytes 1769476
  8.2 5.0 %slice-start.1 = ((s8[4718592]{0:T(1024)(128)(4,1)}), s8[524288]{0:T(1024)(128)(4,1)S(1)}, s32[]{:S(2)}) async-start(s8[4718592]{0:T(1024)(128)(4,1)} %bitcast.118), calls=%async_computation.10 | async-start | bytes 1048576
  13.2 2.5 copy-start.10
  15.8 11.3 %copy-start.11 = (s32[64,8]{0,1:T(8,128)S(1)}, s32[64,8]{0,1:T(8,128)}, u32[]{:S(2)}) copy-start(s32[64,8]{0,1:T(8,128)} %param.26) | copy-start | bytes 6148
  17.4 10.1 %copy-start.15 = (s32[64]{0:T(128)S(1)}, s32[64]{0:T(128)}, u32[]{:S(2)}) copy-start(s32[64]{0:T(128)} %param.28) | copy-start | bytes 772
  18.5 24.6 %all-to-all-start.1 = ((bf16[8,64,512]{2,0,1:T(8,128)(2,1)}), bf16[8,64,512]{2,0,1:T(8,128)(2,1)S(1)}, u32[]{:S(2)}, u32[]{:S(2)}) async-start(bf16[8,64,512]{2,0,1:T(8,128)(2,1)} %copy.75), calls=%async_computation.1 | async-start | bytes 1048576 | tf_op jit(solution)/shard_map/all_to_all | solution.py:111
  27.1 4.5 %copy-start.9 = (bf16[3,1,128,64]{2,3,1,0:T(8,128)(2,1)S(1)}, bf16[3,1,128,64]{2,3,1,0:T(8,128)(2,1)}, u32[]{:S(2)}) copy-start(bf16[3,1,128,64]{2,3,1,0:T(8,128)(2,1)} %param.32) | copy-start | bytes 147460
  31.6 1.5 copy-start.1
  43.1 70.1 %all-to-all-start = ((bf16[16,136,640]{2,1,0:T(8,128)(2,1)}), bf16[16,136,640]{2,1,0:T(8,128)(2,1)}, u32[]{:S(2)}, u32[]{:S(2)}) async-start(bf16[16,136,640]{2,1,0:T(8,128)(2,1)} %copy.72), calls=%async_computation | async-start | bytes 5570560 | tf_op jit(solution)/shard_map/all_to_all | solution.py:73
  50.1 71.1 %all-gather.5.cloned.1.call-start = ((), (), s32[]{:S(2)}) async-start(), calls=%async_computation.6 | async-start | bytes 2228224 | tf_op jit(solution)/shard_map/all_gather | solution.py:118
  124.2 1.3 copy-start.3
  126.5 2.8 collective-permute-start
  126.8 27.9 %copy-start.8 = (bf16[64,448]{1,0:T(8,128)(2,1)S(1)}, bf16[64,448]{1,0:T(8,128)(2,1)}, u32[]{:S(2)}) copy-start(bf16[64,448]{1,0:T(8,128)(2,1)} %param.24) | copy-start | bytes 172036
  154.7 9.2 %copy-start.13 = (bf16[7168]{0:T(1024)(128)(2,1)S(1)}, bf16[7168]{0:T(1024)(128)(2,1)}, u32[]{:S(2)}) copy-start(bf16[7168]{0:T(1024)(128)(2,1)} %param.25) | copy-start | bytes 43012
  154.8 0.6 copy-start.6
  156.5 22.2 %all-to-all-start.3 = ((bf16[16,64,448]{2,1,0:T(8,128)(2,1)}), bf16[16,64,448]{2,1,0:T(8,128)(2,1)}, u32[]{:S(2)}, u32[]{:S(2)}) async-start(bf16[16,64,448]{2,1,0:T(8,128)(2,1)} %broadcast_in_dim.39), calls=%async_computation.3 | async-start | bytes 2097152 | tf_op jit(solution)/shard_map/all_to_all | solution.py:140
  163.6 78.2 %all-gather.7.cloned.1.call-start = ((), (), s32[]{:S(2)}) async-start(), calls=%async_computation.7 | async-start | bytes 9748480 | tf_op jit(solution)/shard_map/all_gather | solution.py:147
  188.6 104.0 %all-gather.9.cloned.1.call-start = ((), (), s32[]{:S(2)}) async-start(), calls=%async_computation.8 | async-start | bytes 2785280 | tf_op jit(solution)/shard_map/all_gather | solution.py:152
  241.8 6.8 %copy-start.16 = (bf16[640,7168]{1,0:T(8,128)(2,1)S(1)}, bf16[640,7168]{1,0:T(8,128)(2,1)}, u32[]{:S(2)}) copy-start(bf16[640,7168]{1,0:T(8,128)(2,1)} %all-gather.7.cloned.1.call-done) | copy-start | bytes 27525124
  241.8 7.2 %copy-start.18 = (bf16[1,7168,128]{2,1,0:T(8,128)(2,1)S(1)}, bf16[1,7168,128]{2,1,0:T(8,128)(2,1)}, u32[]{:S(2)}) copy-start(bf16[1,7168,128]{2,1,0:T(8,128)(2,1)} %param.30) | copy-start | bytes 5505028
  249.1 43.6 %copy-start.4 = (bf16[2048,192]{0,1:T(8,128)(2,1)S(1)}, bf16[2048,192]{0,1:T(8,128)(2,1)}, u32[]{:S(2)}) copy-start(bf16[2048,192]{0,1:T(8,128)(2,1)} %copy.73) | copy-start | bytes 2359300
  292.6 3.8 %copy-start.2 = (bf16[2048,448]{1,0:T(8,128)(2,1)S(1)}, bf16[2048,448]{1,0:T(8,128)(2,1)}, u32[]{:S(2)}) copy-start(bf16[2048,448]{1,0:T(8,128)(2,1)} %slice.41) | copy-start | bytes 5505028
  292.6 3.8 %copy-start.17 = (bf16[10240,128]{1,0:T(8,128)(2,1)S(1)}, bf16[10240,128]{1,0:T(8,128)(2,1)}, u32[]{:S(2)}) copy-start(bf16[10240,128]{1,0:T(8,128)(2,1)} %all-gather.9.cloned.1.call-done) | copy-start | bytes 7864324
  298.9 32.7 %copy-start.12 = (s32[64,8]{0,1:T(8,128)S(1)}, s32[64,8]{0,1:T(8,128)}, u32[]{:S(2)}) copy-start(s32[64,8]{0,1:T(8,128)} %param.26) | copy-start | bytes 6148
  298.9 32.7 %copy-start.14 = (f32[64,8]{0,1:T(8,128)S(1)}, f32[64,8]{0,1:T(8,128)}, u32[]{:S(2)}) copy-start(f32[64,8]{0,1:T(8,128)} %param.27) | copy-start | bytes 6148
  298.9 44.9 %copy-start.7 = (bf16[64,448]{1,0:T(8,128)(2,1)S(1)}, bf16[64,448]{1,0:T(8,128)(2,1)}, u32[]{:S(2)}) copy-start(bf16[64,448]{1,0:T(8,128)(2,1)} %copy-done.6) | copy-start | bytes 172036
  324.8 19.0 %all-to-all-start.5 = ((bf16[16,40,448]{2,1,0:T(8,128)(2,1)}), bf16[16,40,448]{2,1,0:T(8,128)(2,1)S(1)}, u32[]{:S(2)}, u32[]{:S(2)}) async-start(bf16[16,40,448]{2,1,0:T(8,128)(2,1)} %all_to_all.44), calls=%async_computation.5 | async-start | bytes 1310720 | tf_op jit(solution)/shard_map/all_to_all | solution.py:166
Sparse Core Ops, SparseCore 0:
  53.3 51.1 all-gather.4
  188.7 53.0 all-gather.6
  252.4 40.1 all-gather.8

commit v5 on v4

--- a/solution.py
+++ b/solution.py
@@ -62,9 +62,9 @@
     down_local = jnp.transpose(down_local, (1, 0, 2))
     left_local = left_delta_factor[:, 0]
     tenants, _, rank = left_local.shape
-    left_local = jnp.transpose(left_local, (1, 0, 2)).reshape(1, hidden_slice, tenants * rank)
-    left_local = jnp.broadcast_to(left_local, (n_slices, hidden_slice, tenants * rank))
-    down_pack = jnp.concatenate([down_local, left_local], axis=2)
+    left_local = jnp.transpose(left_local, (1, 0, 2)).reshape(hidden_slice, tenants * rank)
+    left_all = lax.all_gather(left_local, RT, axis=0, tiled=True)
+    down_pack = down_local
     pack_width = down_pack.shape[2]
     info = mine_owner.astype(jnp.bfloat16)
     info_rows = jnp.zeros((8, pack_width), jnp.bfloat16).at[0, : info.shape[0]].set(info)
@@ -119,7 +119,7 @@
     owners = down_pack[:, hidden_slice, :capacity].astype(jnp.int32).reshape(n_slices * capacity)
     down_pack = down_pack[:, :hidden_slice].reshape(n_slices * hidden_slice, pack_width)
     down_w = down_pack[:, :col_width]
-    left_w = down_pack[:, col_width:].reshape(n_slices * hidden_slice, tenants, rank)
+    left_w = left_all.reshape(n_slices * hidden_slice, tenants, rank)
     down_w, left_w, owners, all_values = lax.optimization_barrier((down_w, left_w, owners, all_values))
     partial = jnp.dot(all_values, out_proj, preferred_element_type=jnp.float32)
     half = partial.shape[0] // 2

time: 353 us -> 381 us (1.079)
  blocking collectives: 46.3 us -> 128 us
  waiting for transfers between devices: 183 us -> 135 us
    all_gather x0 -> x1, blocking collectives: none -> 78.8 us  [local(): left_all = lax.all_gather(left_local, RT, axis=0, tiled=True)]
    all_to_all x1, waiting for transfers between devices: 60.9 us -> 0.01 us  [local(): lax.all_to_all(down_pack, RT, split_axis=0, concat_axis=0, tiled=True)]
    all_to_all x1, waiting for transfers between devices: 0.29 us -> 11.2 us  [local(): lax.all_to_all(attended, 'tensor', split_axis=1, concat_axis=0, tiled=True)]
    slice x3 -> x0, local copies, waits for them, and re-layouts: 5.1 us -> none  [the longest x2 3.62 us: local(): down_pack[:, col_width:].reshape(n_slices * hidden_slice, tenants, rank)]
    reshape x0 -> x1, local copies, waits for them, and re-layouts: none -> 3.91 us  [local(): down_pack[:, :hidden_slice].reshape(n_slices * hidden_slice, pack_width)]
  transfers between devices with their start and end apart: 8 -> 8, of which waited for: 7 -> 6; matrix products, arithmetic and copies ran while one was open for 7% -> 5% of each run, Pallas kernels for 0% -> 0%
where the time goes in v5:
time: 381 us; the launch traced here: 379 us
  waiting for transfers between devices  135 us (35%)
  blocking collectives  128 us (34%)
  matrix products  33.1 us (9%)
  local copies, waits for them, and re-layouts  31.1 us (8%)
  starting transfers between devices  28.5 us (7%)
  between operations  13.5 us (4%)
  other arithmetic  11 us (3%)
    all_gather x1, blocking collectives, local(): left_all = lax.all_gather(left_local, RT, axis=0, tiled=True)  78.8 us
    all_gather x1, waiting for transfers between devices, local(): collected_rows = lax.all_gather(picked, RT, axis=0, tiled=True)  53.2 us
    all_gather x1, waiting for transfers between devices, local(): gathered = lax.all_gather(hidden, RT, axis=0, tiled=False)  40.3 us
    all_to_all x1, blocking collectives, local(): lax.all_to_all(expert_out, RT, split_axis=0, concat_axis=0, tiled=True)  24.5 us
    all_to_all x1, blocking collectives, local(): lax.all_to_all(partial.astype(jnp.bfloat16), 'tensor', split_axis=0, conc...  24.5 us
    all_to_all x1, waiting for transfers between devices, local(): lax.all_to_all(spread, 'dp', split_axis=0, concat_axis=0, tiled=True)  14.8 us
    all_to_all x1, waiting for transfers between devices, local(): lax.all_to_all(by_group, 'dp', split_axis=0, concat_axis=0, tiled=True)  12.1 us
    all_to_all x1, waiting for transfers between devices, local(): lax.all_to_all(attended, 'tensor', split_axis=1, concat_axis=0, tiled=True)  11.2 us
  transfers between devices with their start and end apart: 8, of which 6 were waited for; matrix products, arithmetic and copies ran while one was open for 5% of the time, Pallas kernels for 0%

profile of v5, /device:TPU:32, one launch (start us, length us, event | category | flops | bytes accessed | tf_op | source)
XLA Modules:
  0.0 379.4 jit_solution(3406468064645977687)
XLA Ops:
  6.5 0.9 iota_compare_fusion.3
  7.4 0.7 reshape.196
  8.2 3.9 %fusion.8 = (f32[4,2,64]{2,1,0:T(2,128)S(1)}, f32[4,2,64,1024]{3,2,1,0:T(8,128)S(1)}) fusion(pred[4,1024]{1,0:T(4,128)(4,1)S(1)} %iota_compare_fusion.3, bf16[4,2,64,576]{3,2,1,0:T(8,128)(2,1)} %bitcast.130, bf16[4,1024,576]{1,2,0:T(8,128)(2,1)} %param.19), kind=kOutput, calls=%fused_computation.14 | convolution fusion | flops 605552128 | bytes 7411712 | tf_op jit(solution)/shard_map/sqhd,spd->sqhp/dot_general | solution.py:80
  12.1 0.4 fusion.68
  12.6 0.6 fusion.16
  13.2 2.5 fusion.2
  15.8 1.6 fusion.24
  17.4 1.1 copy.81
  18.5 8.6 %all-to-all-start.1 = ((bf16[8,64,512]{2,0,1:T(8,128)(2,1)}), bf16[8,64,512]{2,0,1:T(8,128)(2,1)S(1)}, u32[]{:S(2)}, u32[]{:S(2)}) async-start(bf16[8,64,512]{2,0,1:T(8,128)(2,1)} %copy.81), calls=%async_computation.1 | async-start | bytes 1048576 | tf_op jit(solution)/shard_map/all_to_all | solution.py:111
  27.1 0.2 reduce_window_sum.11
  27.3 0.1 fusion.47
  27.4 0.1 select_reduce_fusion.1
  27.6 0.1 copy.96
  27.7 0.0 copy-done.10
  27.7 0.2 copy-done.5
  27.9 3.9 %copy.76 = bf16[1,128,7168]{1,2,0:T(8,128)(2,1)} copy(bf16[1,128,7168]{2,1,0:T(8,128)(2,1)} %param.31) | data formatting | bytes 3670016 | tf_op args[13]
  31.8 11.2 %all-to-all-done.1 = bf16[8,64,512]{2,0,1:T(8,128)(2,1)S(1)} async-done(((bf16[8,64,512]{2,0,1:T(8,128)(2,1)}), bf16[8,64,512]{2,0,1:T(8,128)(2,1)S(1)}, u32[]{:S(2)}, u32[]{:S(2)}) %all-to-all-start.1) | async-done | bytes 524320 | tf_op jit(solution)/shard_map/all_to_all | solution.py:111
  43.1 1.5 fusion.33
  44.6 0.7 copy.115
  45.3 0.0 all-gather.5.cloned.1.call-update
  45.3 0.3 broadcast_in_dim.24
  45.7 1.1 copy-done.1
  46.8 2.6 pad_maximum_fusion
  49.4 4.7 %copy.78 = bf16[16,136,448]{2,1,0:T(8,128)(2,1)} copy(bf16[16,136,448]{1,2,0:T(8,128)(2,1)} %pad_maximum_fusion) | data formatting | bytes 3899392 | tf_op jit(solution)/shard_map/concatenate | solution.py:72
  54.1 5.8 %all-to-all-start = ((bf16[16,136,448]{2,1,0:T(8,128)(2,1)}), bf16[16,136,448]{2,1,0:T(8,128)(2,1)}, u32[]{:S(2)}, u32[]{:S(2)}) async-start(bf16[16,136,448]{2,1,0:T(8,128)(2,1)} %copy.78), calls=%async_computation | async-start | bytes 4456448 | tf_op jit(solution)/shard_map/all_to_all | solution.py:73
  59.9 78.8 %all_gather.15 = bf16[2048,192]{0,1:T(8,128)(2,1)} all-gather(bf16[128,192]{0,1:T(8,128)(2,1)S(1)} %bitcast.134), channel_id=1, replica_groups=mesh['role'=2,'dp'=16,'tensor'=8] {'role','tensor'}, dimensions={0}, use_global_device_ids=true | all-gather | bytes 835584 | tf_op jit(solution)/shard_map/all_gather | solution.py:66
  138.6 3.1 slice.32
  141.7 3.9 %copy.94 = bf16[2048,448]{0,1:T(8,128)(2,1)} copy(bf16[2048,448]{1,0:T(8,128)(2,1)} %bitcast.122) | data formatting | bytes 3670016 | tf_op jit(solution)/shard_map/reshape | solution.py:120
  145.6 0.8 fusion.57
  146.4 0.1 reshape.192
  146.5 0.0 all-gather.5.cloned.1.call-done
  146.5 3.0 fusion.69
  149.5 1.2 copy-done.2
  150.8 1.0 constant_dynamic-slice_fusion
  151.8 2.8 collective-permute-done
  154.6 2.4 add_convert_fusion
  157.0 1.2 copy.84
  158.2 24.5 %all_to_all.43 = bf16[8,64,448]{2,1,0:T(8,128)(2,1)S(1)} all-to-all(bf16[8,64,448]{2,1,0:T(8,128)(2,1)S(1)} %bitcast.128), channel_id=1, replica_groups=mesh['role'=2,'dp'=16,'tensor'=8] {'tensor'}, dimensions={0} | all-to-all | bytes 917504 | tf_op jit(solution)/shard_map/all_to_all | solution.py:132
  182.7 0.1 convert_reduce_fusion
  182.8 1.1 broadcast_in_dim.33
  183.9 7.1 %all-to-all-start.3 = ((bf16[16,64,448]{2,1,0:T(8,128)(2,1)}), bf16[16,64,448]{2,1,0:T(8,128)(2,1)}, u32[]{:S(2)}, u32[]{:S(2)}) async-start(bf16[16,64,448]{2,1,0:T(8,128)(2,1)} %broadcast_in_dim.33), calls=%async_computation.3 | async-start | bytes 2097152 | tf_op jit(solution)/shard_map/all_to_all | solution.py:140
  191.1 0.2 all-gather.7.cloned.1.call-start
  191.3 0.1 reshape.193
  191.4 14.8 %all-to-all-done.3 = bf16[16,64,448]{2,1,0:T(8,128)(2,1)} async-done(((bf16[16,64,448]{2,1,0:T(8,128)(2,1)}), bf16[16,64,448]{2,1,0:T(8,128)(2,1)}, u32[]{:S(2)}, u32[]{:S(2)}) %all-to-all-start.3) | async-done | bytes 917536 | tf_op jit(solution)/shard_map/all_to_all | solution.py:140
  206.1 1.6 fusion.5
  207.7 1.6 fusion.37
  209.3 1.6 copy.85
  210.8 2.9 convert_element_type.125
  213.7 2.3 convolution_convert_fusion
  216.0 0.0 all-gather.7.cloned.1.call-update
  216.1 0.0 all-gather.9.cloned.1.call-start
  216.1 53.2 %all-gather.7.cloned.1.call-done = bf16[640,7168]{1,0:T(8,128)(2,1)} async-done(((bf16[40,7168]{1,0:T(8,128)(2,1)}), bf16[640,7168]{1,0:T(8,128)(2,1)}) %all-gather.7.cloned.1.call-update) | async-done | bytes 9175056 | tf_op jit(solution)/shard_map/all_gather | solution.py:147
  269.3 6.8 %fusion.14 = f32[640,128]{1,0:T(8,128)S(1)} fusion(bf16[640,7168]{1,0:T(8,128)(2,1)} %all-gather.7.cloned.1.call-done, bf16[1,7168,128]{2,1,0:T(8,128)(2,1)} %param.29), kind=kOutput, calls=%fused_computation.20 | convolution fusion | flops 1174405120 | bytes 11337728 | tf_op jit(solution)/shard_map/dot_general | solution.py:148
  276.1 0.4 copy-done.19
  276.5 3.2 fusion.29
  279.8 40.3 %all-gather.9.cloned.1.call-done = bf16[10240,128]{1,0:T(8,128)(2,1)} async-done(((bf16[640,128]{1,0:T(8,128)(2,1)}), bf16[10240,128]{1,0:T(8,128)(2,1)}) %all-gather.9.cloned.1.call-update) | async-done | bytes 2621456 | tf_op jit(solution)/shard_map/all_gather | solution.py:152
  320.1 4.1 %fusion.18 = f32[640,448]{0,1:T(8,128)S(1)} fusion(bf16[16,640,128]{2,1,0:T(8,128)(2,1)} %bitcast.136, bf16[2048,448]{0,1:T(8,128)(2,1)} %copy.94), kind=kOutput, calls=%fused_computation.24 | convolution fusion | flops 1174405120 | bytes 5603328 | tf_op jit(solution)/shard_map/jsh,jhc->sc/dot_general | solution.py:155
  324.2 1.0 fusion.25
  325.2 1.7 fusion.23
  326.9 1.3 copy.88
  328.2 24.5 %all_to_all.44 = bf16[16,40,448]{2,1,0:T(8,128)(2,1)} all-to-all(bf16[16,40,448]{2,1,0:T(8,128)(2,1)S(1)} %bitcast.126), channel_id=1, replica_groups=mesh['role'=2,'dp'=16,'tensor'=8] {'role','tensor'}, dimensions={0} | all-to-all | bytes 1146880 | tf_op jit(solution)/shard_map/all_to_all | solution.py:165
  352.8 6.8 %all-to-all-start.5 = ((bf16[16,40,448]{2,1,0:T(8,128)(2,1)}), bf16[16,40,448]{2,1,0:T(8,128)(2,1)S(1)}, u32[]{:S(2)}, u32[]{:S(2)}) async-start(bf16[16,40,448]{2,1,0:T(8,128)(2,1)} %all_to_all.44), calls=%async_computation.5 | async-start | bytes 1310720 | tf_op jit(solution)/shard_map/all_to_all | solution.py:166
  359.6 12.1 %all-to-all-done.5 = bf16[16,40,448]{2,1,0:T(8,128)(2,1)S(1)} async-done(((bf16[16,40,448]{2,1,0:T(8,128)(2,1)}), bf16[16,40,448]{2,1,0:T(8,128)(2,1)S(1)}, u32[]{:S(2)}, u32[]{:S(2)}) %all-to-all-start.5) | async-done | bytes 573472 | tf_op jit(solution)/shard_map/all_to_all | solution.py:166
  371.8 1.1 fusion.34
  (58 shorter events, 0.3 us)
Async XLA Ops:
  6.5 318.7 %copy-start = (bf16[3,1,64,7168]{3,2,1,0:T(8,128)(2,1)S(1)}, bf16[3,1,64,7168]{3,2,1,0:T(8,128)(2,1)}, u32[]{:S(2)}) copy-start(bf16[3,1,64,7168]{3,2,1,0:T(8,128)(2,1)} %param.33) | copy-start | bytes 8257540
  8.1 5.0 %slice-start = ((s8[4718592]{0:T(1024)(128)(4,1)}), s8[4194304]{0:T(1024)(128)(4,1)S(1)}, s32[]{:S(2)}) async-start(s8[4718592]{0:T(1024)(128)(4,1)} %bitcast.124), calls=%async_computation.9 | async-start | bytes 8388608
  8.1 4.0 %copy-start.4 = (bf16[8,64,576]{2,1,0:T(8,128)(2,1)S(1)}, bf16[8,64,576]{2,1,0:T(8,128)(2,1)}, u32[]{:S(2)}) copy-start(bf16[8,64,576]{2,1,0:T(8,128)(2,1)} %param.18) | copy-start | bytes 1769476
  8.2 5.0 %slice-start.1 = ((s8[4718592]{0:T(1024)(128)(4,1)}), s8[524288]{0:T(1024)(128)(4,1)S(1)}, s32[]{:S(2)}) async-start(s8[4718592]{0:T(1024)(128)(4,1)} %bitcast.124), calls=%async_computation.10 | async-start | bytes 1048576
  13.2 2.5 copy-start.9
  15.8 11.3 %copy-start.12 = (s32[64,8]{0,1:T(8,128)S(1)}, s32[64,8]{0,1:T(8,128)}, u32[]{:S(2)}) copy-start(s32[64,8]{0,1:T(8,128)} %param.26) | copy-start | bytes 6148
  17.4 10.0 %copy-start.16 = (s32[64]{0:T(128)S(1)}, s32[64]{0:T(128)}, u32[]{:S(2)}) copy-start(s32[64]{0:T(128)} %param.28) | copy-start | bytes 772
  18.5 24.6 %all-to-all-start.1 = ((bf16[8,64,512]{2,0,1:T(8,128)(2,1)}), bf16[8,64,512]{2,0,1:T(8,128)(2,1)S(1)}, u32[]{:S(2)}, u32[]{:S(2)}) async-start(bf16[8,64,512]{2,0,1:T(8,128)(2,1)} %copy.81), calls=%async_computation.1 | async-start | bytes 1048576 | tf_op jit(solution)/shard_map/all_to_all | solution.py:111
  27.1 119.5 %all-gather.5.cloned.1.call-start = ((), (), s32[]{:S(2)}) async-start(), calls=%async_computation.6 | async-start | bytes 2228224 | tf_op jit(solution)/shard_map/all_gather | solution.py:118
  27.1 0.6 copy-start.10
  27.3 0.6 copy-start.5
  45.3 1.5 copy-start.1
  54.1 5.8 %copy-start.8 = (bf16[3,1,128,64]{2,3,1,0:T(8,128)(2,1)S(1)}, bf16[3,1,128,64]{2,3,1,0:T(8,128)(2,1)}, u32[]{:S(2)}) copy-start(bf16[3,1,128,64]{2,3,1,0:T(8,128)(2,1)} %param.32) | copy-start | bytes 147460
  54.1 84.5 %all-to-all-start = ((bf16[16,136,448]{2,1,0:T(8,128)(2,1)}), bf16[16,136,448]{2,1,0:T(8,128)(2,1)}, u32[]{:S(2)}, u32[]{:S(2)}) async-start(bf16[16,136,448]{2,1,0:T(8,128)(2,1)} %copy.78), calls=%async_computation | async-start | bytes 4456448 | tf_op jit(solution)/shard_map/all_to_all | solution.py:73
  149.5 1.3 copy-start.2
  151.8 2.8 collective-permute-start
  151.8 31.0 %copy-start.7 = (bf16[64,448]{1,0:T(8,128)(2,1)S(1)}, bf16[64,448]{1,0:T(8,128)(2,1)}, u32[]{:S(2)}) copy-start(bf16[64,448]{1,0:T(8,128)(2,1)} %param.24) | copy-start | bytes 172036
  182.7 8.6 %copy-start.14 = (bf16[7168]{0:T(1024)(128)(2,1)S(1)}, bf16[7168]{0:T(1024)(128)(2,1)}, u32[]{:S(2)}) copy-start(bf16[7168]{0:T(1024)(128)(2,1)} %param.25) | copy-start | bytes 43012
  183.9 22.2 %all-to-all-start.3 = ((bf16[16,64,448]{2,1,0:T(8,128)(2,1)}), bf16[16,64,448]{2,1,0:T(8,128)(2,1)}, u32[]{:S(2)}, u32[]{:S(2)}) async-start(bf16[16,64,448]{2,1,0:T(8,128)(2,1)} %broadcast_in_dim.33), calls=%async_computation.3 | async-start | bytes 2097152 | tf_op jit(solution)/shard_map/all_to_all | solution.py:140
  191.1 78.2 %all-gather.7.cloned.1.call-start = ((), (), s32[]{:S(2)}) async-start(), calls=%async_computation.7 | async-start | bytes 9748480 | tf_op jit(solution)/shard_map/all_gather | solution.py:147
  216.1 104.0 %all-gather.9.cloned.1.call-start = ((), (), s32[]{:S(2)}) async-start(), calls=%async_computation.8 | async-start | bytes 2785280 | tf_op jit(solution)/shard_map/all_gather | solution.py:152
  269.3 6.8 %copy-start.17 = (bf16[640,7168]{1,0:T(8,128)(2,1)S(1)}, bf16[640,7168]{1,0:T(8,128)(2,1)}, u32[]{:S(2)}) copy-start(bf16[640,7168]{1,0:T(8,128)(2,1)} %all-gather.7.cloned.1.call-done) | copy-start | bytes 27525124
  269.3 7.2 %copy-start.19 = (bf16[1,7168,128]{2,1,0:T(8,128)(2,1)S(1)}, bf16[1,7168,128]{2,1,0:T(8,128)(2,1)}, u32[]{:S(2)}) copy-start(bf16[1,7168,128]{2,1,0:T(8,128)(2,1)} %param.30) | copy-start | bytes 5505028
  320.1 4.1 %copy-start.3 = (bf16[2048,192]{0,1:T(8,128)(2,1)S(1)}, bf16[2048,192]{0,1:T(8,128)(2,1)}, u32[]{:S(2)}) copy-start(bf16[2048,192]{0,1:T(8,128)(2,1)} %all_gather.15) | copy-start | bytes 2359300
  320.1 4.1 %copy-start.18 = (bf16[10240,128]{1,0:T(8,128)(2,1)S(1)}, bf16[10240,128]{1,0:T(8,128)(2,1)}, u32[]{:S(2)}) copy-start(bf16[10240,128]{1,0:T(8,128)(2,1)} %all-gather.9.cloned.1.call-done) | copy-start | bytes 7864324
  326.9 32.7 %copy-start.13 = (s32[64,8]{0,1:T(8,128)S(1)}, s32[64,8]{0,1:T(8,128)}, u32[]{:S(2)}) copy-start(s32[64,8]{0,1:T(8,128)} %param.26) | copy-start | bytes 6148
  326.9 32.7 %copy-start.15 = (f32[64,8]{0,1:T(8,128)S(1)}, f32[64,8]{0,1:T(8,128)}, u32[]{:S(2)}) copy-start(f32[64,8]{0,1:T(8,128)} %param.27) | copy-start | bytes 6148
  326.9 44.9 %copy-start.6 = (s32[16,64]{1,0:T(8,128)S(1)}, s32[16,64]{1,0:T(8,128)}, u32[]{:S(2)}) copy-start(s32[16,64]{1,0:T(8,128)} %copy-done.5) | copy-start | bytes 12292
  326.9 44.9 %copy-start.11 = (pred[16,64]{1,0:T(8,128)(4,1)S(1)}, pred[16,64]{1,0:T(8,128)(4,1)}, u32[]{:S(2)}) copy-start(pred[16,64]{1,0:T(8,128)(4,1)} %copy-done.10) | copy-start | bytes 3076
  352.8 19.0 %all-to-all-start.5 = ((bf16[16,40,448]{2,1,0:T(8,128)(2,1)}), bf16[16,40,448]{2,1,0:T(8,128)(2,1)S(1)}, u32[]{:S(2)}, u32[]{:S(2)}) async-start(bf16[16,40,448]{2,1,0:T(8,128)(2,1)} %all_to_all.44), calls=%async_computation.5 | async-start | bytes 1310720 | tf_op jit(solution)/shard_map/all_to_all | solution.py:166
Sparse Core Ops, SparseCore 0:
  45.5 47.2 all-gather.4
  216.2 53.0 all-gather.6
  279.9 40.1 all-gather.8

commit v6 on v4

--- a/solution.py
+++ b/solution.py
@@ -126,7 +126,7 @@
     role_idx = lax.axis_index("role")
     keep = lax.dynamic_slice_in_dim(partial, role_idx * half, half, 0)
     give = lax.dynamic_slice_in_dim(partial, (1 - role_idx) * half, half, 0)
-    partial = keep + lax.ppermute(give, "role", [(0, 1), (1, 0)])
+    partial = keep + lax.ppermute(give.astype(jnp.bfloat16), "role", [(0, 1), (1, 0)]).astype(jnp.float32)
     n_tensor = lax.axis_size("tensor")
     partial = partial.reshape(n_tensor, partial.shape[0] // n_tensor, partial.shape[1])
     partial = lax.all_to_all(partial.astype(jnp.bfloat16), "tensor", split_axis=0, concat_axis=0, tiled=True)

time: 353 us -> 351 us (level)
  no operation moved by 1% of the time
where the time goes in v6:
time: 351 us; the launch traced here: 350 us
  waiting for transfers between devices  183 us (52%)
  blocking collectives  46.3 us (13%)
  matrix products  32.5 us (9%)
  local copies, waits for them, and re-layouts  32.1 us (9%)
  starting transfers between devices  30.2 us (9%)
  between operations  13.5 us (4%)
  other arithmetic  12.3 us (4%)
    all_to_all x1, waiting for transfers between devices, local(): lax.all_to_all(down_pack, RT, split_axis=0, concat_axis=0, tiled=True)  60.9 us
    all_gather x1, waiting for transfers between devices, local(): collected_rows = lax.all_gather(picked, RT, axis=0, tiled=True)  53.2 us
    all_gather x1, waiting for transfers between devices, local(): gathered = lax.all_gather(hidden, RT, axis=0, tiled=False)  39.7 us
    all_to_all x1, blocking collectives, local(): lax.all_to_all(expert_out, RT, split_axis=0, concat_axis=0, tiled=True)  24.5 us
    all_to_all x1, blocking collectives, local(): lax.all_to_all(partial.astype(jnp.bfloat16), 'tensor', split_axis=0, conc...  21.8 us
    all_to_all x1, waiting for transfers between devices, local(): lax.all_to_all(spread, 'dp', split_axis=0, concat_axis=0, tiled=True)  14.8 us
    all_to_all x1, waiting for transfers between devices, local(): lax.all_to_all(by_group, 'dp', split_axis=0, concat_axis=0, tiled=True)  12.1 us
    all_to_all x1, starting transfers between devices, local(): lax.all_to_all(attended, 'tensor', split_axis=1, concat_axis=0, tiled=True)  8.57 us
  transfers between devices with their start and end apart: 8, of which 7 were waited for; matrix products, arithmetic and copies ran while one was open for 7% of the time, Pallas kernels for 0%

profile of v6, /device:TPU:32, one launch (start us, length us, event | category | flops | bytes accessed | tf_op | source)
XLA Modules:
  0.0 349.5 jit_solution(5170644350469607524)
XLA Ops:
  6.5 0.9 iota_compare_fusion.3
  7.4 0.7 reshape.194
  8.2 3.9 %fusion.8 = (f32[4,2,64]{2,1,0:T(2,128)S(1)}, f32[4,2,64,1024]{3,2,1,0:T(8,128)S(1)}) fusion(pred[4,1024]{1,0:T(4,128)(4,1)S(1)} %iota_compare_fusion.3, bf16[4,2,64,576]{3,2,1,0:T(8,128)(2,1)} %bitcast.125, bf16[4,1024,576]{1,2,0:T(8,128)(2,1)} %param.19), kind=kOutput, calls=%fused_computation.14 | convolution fusion | flops 605552128 | bytes 7411712 | tf_op jit(solution)/shard_map/sqhd,spd->sqhp/dot_general | solution.py:80
  12.1 0.4 fusion.62
  12.6 0.6 fusion.13
  13.2 2.5 fusion.2
  15.8 1.6 fusion.18
  17.4 1.1 copy.75
  18.5 8.6 %all-to-all-start.1 = ((bf16[8,64,512]{2,0,1:T(8,128)(2,1)}), bf16[8,64,512]{2,0,1:T(8,128)(2,1)S(1)}, u32[]{:S(2)}, u32[]{:S(2)}) async-start(bf16[8,64,512]{2,0,1:T(8,128)(2,1)} %copy.75), calls=%async_computation.1 | async-start | bytes 1048576 | tf_op jit(solution)/shard_map/all_to_all | solution.py:111
  27.2 0.2 reduce_window_sum.11
  27.4 0.1 fusion.41
  27.5 0.1 select_reduce_fusion.1
  27.6 0.1 copy.92
  27.7 3.9 %copy.70 = bf16[1,128,7168]{1,2,0:T(8,128)(2,1)} copy(bf16[1,128,7168]{2,1,0:T(8,128)(2,1)} %param.31) | data formatting | bytes 3670016 | tf_op args[13]
  31.7 0.5 broadcast_in_dim.30
  32.2 0.9 copy-done.1
  33.1 3.5 pad_maximum_fusion
  36.6 6.3 %copy.72 = bf16[16,136,640]{2,1,0:T(8,128)(2,1)} copy(bf16[16,136,640]{1,2,0:T(8,128)(2,1)} %pad_maximum_fusion) | data formatting | bytes 5570560 | tf_op jit(solution)/shard_map/concatenate | solution.py:72
  42.8 0.3 all-to-all-done.1
  43.1 6.9 %all-to-all-start = ((bf16[16,136,640]{2,1,0:T(8,128)(2,1)}), bf16[16,136,640]{2,1,0:T(8,128)(2,1)}, u32[]{:S(2)}, u32[]{:S(2)}) async-start(bf16[16,136,640]{2,1,0:T(8,128)(2,1)} %copy.72), calls=%async_computation | async-start | bytes 5570560 | tf_op jit(solution)/shard_map/all_to_all | solution.py:73
  50.1 1.5 fusion.27
  51.7 0.7 copy.104
  52.4 60.9 %all-to-all-done = bf16[16,136,640]{2,1,0:T(8,128)(2,1)} async-done(((bf16[16,136,640]{2,1,0:T(8,128)(2,1)}), bf16[16,136,640]{2,1,0:T(8,128)(2,1)}, u32[]{:S(2)}, u32[]{:S(2)}) %all-to-all-start) | async-done | bytes 2785312 | tf_op jit(solution)/shard_map/all_to_all | solution.py:73
  113.2 2.0 slice.40
  115.2 1.5 slice.41
  116.7 1.4 slice.42
  118.1 2.2 copy.73
  120.3 0.8 fusion.51
  121.1 0.1 reshape.190
  121.2 3.0 fusion.63
  124.2 1.2 copy-done.3
  125.4 0.1 dynamic-slice_convert_fusion
  125.5 0.5 collective-permute-start
  126.0 1.6 collective-permute-done
  127.6 2.2 add_convert_fusion
  129.8 1.2 copy.78
  131.0 21.8 %all_to_all.43 = bf16[8,64,448]{2,1,0:T(8,128)(2,1)S(1)} all-to-all(bf16[8,64,448]{2,1,0:T(8,128)(2,1)S(1)} %bitcast.123), channel_id=1, replica_groups=mesh['role'=2,'dp'=16,'tensor'=8] {'tensor'}, dimensions={0} | all-to-all | bytes 917504 | tf_op jit(solution)/shard_map/all_to_all | solution.py:132
  152.8 0.1 convert_reduce_fusion
  152.9 0.6 copy-done.6
  153.5 1.1 broadcast_in_dim.39
  154.6 7.1 %all-to-all-start.3 = ((bf16[16,64,448]{2,1,0:T(8,128)(2,1)}), bf16[16,64,448]{2,1,0:T(8,128)(2,1)}, u32[]{:S(2)}, u32[]{:S(2)}) async-start(bf16[16,64,448]{2,1,0:T(8,128)(2,1)} %broadcast_in_dim.39), calls=%async_computation.3 | async-start | bytes 2097152 | tf_op jit(solution)/shard_map/all_to_all | solution.py:140
  161.7 0.2 all-gather.7.cloned.1.call-start
  162.0 0.1 reshape.191
  162.0 14.8 %all-to-all-done.3 = bf16[16,64,448]{2,1,0:T(8,128)(2,1)} async-done(((bf16[16,64,448]{2,1,0:T(8,128)(2,1)}), bf16[16,64,448]{2,1,0:T(8,128)(2,1)}, u32[]{:S(2)}, u32[]{:S(2)}) %all-to-all-start.3) | async-done | bytes 917536 | tf_op jit(solution)/shard_map/all_to_all | solution.py:140
  176.8 1.6 fusion.5
  178.4 1.6 fusion.31
  179.9 1.5 copy.79
  181.5 2.9 convert_element_type.133
  184.4 2.3 convolution_convert_fusion
  186.7 0.0 all-gather.9.cloned.1.call-start
  186.8 53.2 %all-gather.7.cloned.1.call-done = bf16[640,7168]{1,0:T(8,128)(2,1)} async-done(((bf16[40,7168]{1,0:T(8,128)(2,1)}), bf16[640,7168]{1,0:T(8,128)(2,1)}) %all-gather.7.cloned.1.call-update) | async-done | bytes 9175056 | tf_op jit(solution)/shard_map/all_gather | solution.py:147
  239.9 6.8 %fusion.11 = f32[640,128]{1,0:T(8,128)S(1)} fusion(bf16[640,7168]{1,0:T(8,128)(2,1)} %all-gather.7.cloned.1.call-done, bf16[1,7168,128]{2,1,0:T(8,128)(2,1)} %param.29), kind=kOutput, calls=%fused_computation.17 | convolution fusion | flops 1174405120 | bytes 11337728 | tf_op jit(solution)/shard_map/dot_general | solution.py:148
  246.7 0.4 copy-done.18
  247.2 3.2 fusion.23
  250.4 0.6 fusion.50
  251.0 39.7 %all-gather.9.cloned.1.call-done = bf16[10240,128]{1,0:T(8,128)(2,1)} async-done(((bf16[640,128]{1,0:T(8,128)(2,1)}), bf16[10240,128]{1,0:T(8,128)(2,1)}) %all-gather.9.cloned.1.call-update) | async-done | bytes 2621456 | tf_op jit(solution)/shard_map/all_gather | solution.py:152
  290.8 2.9 fusion.19
  293.7 0.8 convolution_bitcast_fusion
  294.5 2.4 fusion.17
  297.0 1.3 copy.83
  298.3 24.5 %all_to_all.44 = bf16[16,40,448]{2,1,0:T(8,128)(2,1)} all-to-all(bf16[16,40,448]{2,1,0:T(8,128)(2,1)S(1)} %bitcast.120), channel_id=1, replica_groups=mesh['role'=2,'dp'=16,'tensor'=8] {'role','tensor'}, dimensions={0} | all-to-all | bytes 1146880 | tf_op jit(solution)/shard_map/all_to_all | solution.py:165
  322.9 6.8 %all-to-all-start.5 = ((bf16[16,40,448]{2,1,0:T(8,128)(2,1)}), bf16[16,40,448]{2,1,0:T(8,128)(2,1)S(1)}, u32[]{:S(2)}, u32[]{:S(2)}) async-start(bf16[16,40,448]{2,1,0:T(8,128)(2,1)} %all_to_all.44), calls=%async_computation.5 | async-start | bytes 1310720 | tf_op jit(solution)/shard_map/all_to_all | solution.py:166
  329.7 12.1 %all-to-all-done.5 = bf16[16,40,448]{2,1,0:T(8,128)(2,1)S(1)} async-done(((bf16[16,40,448]{2,1,0:T(8,128)(2,1)}), bf16[16,40,448]{2,1,0:T(8,128)(2,1)S(1)}, u32[]{:S(2)}, u32[]{:S(2)}) %all-to-all-start.5) | async-done | bytes 573472 | tf_op jit(solution)/shard_map/all_to_all | solution.py:166
  341.9 1.1 fusion.28
  (58 shorter events, 0.4 us)
Async XLA Ops:
  6.5 287.1 %copy-start = (bf16[3,1,64,7168]{3,2,1,0:T(8,128)(2,1)S(1)}, bf16[3,1,64,7168]{3,2,1,0:T(8,128)(2,1)}, u32[]{:S(2)}) copy-start(bf16[3,1,64,7168]{3,2,1,0:T(8,128)(2,1)} %param.33) | copy-start | bytes 8257540
  8.1 5.0 %slice-start = ((s8[4718592]{0:T(1024)(128)(4,1)}), s8[4194304]{0:T(1024)(128)(4,1)S(1)}, s32[]{:S(2)}) async-start(s8[4718592]{0:T(1024)(128)(4,1)} %bitcast.118), calls=%async_computation.9 | async-start | bytes 8388608
  8.1 4.0 %copy-start.5 = (bf16[8,64,576]{2,1,0:T(8,128)(2,1)S(1)}, bf16[8,64,576]{2,1,0:T(8,128)(2,1)}, u32[]{:S(2)}) copy-start(bf16[8,64,576]{2,1,0:T(8,128)(2,1)} %param.18) | copy-start | bytes 1769476
  8.2 5.0 %slice-start.1 = ((s8[4718592]{0:T(1024)(128)(4,1)}), s8[524288]{0:T(1024)(128)(4,1)S(1)}, s32[]{:S(2)}) async-start(s8[4718592]{0:T(1024)(128)(4,1)} %bitcast.118), calls=%async_computation.10 | async-start | bytes 1048576
  13.2 2.5 copy-start.10
  15.8 11.3 %copy-start.11 = (s32[64,8]{0,1:T(8,128)S(1)}, s32[64,8]{0,1:T(8,128)}, u32[]{:S(2)}) copy-start(s32[64,8]{0,1:T(8,128)} %param.26) | copy-start | bytes 6148
  17.4 10.1 %copy-start.15 = (s32[64]{0:T(128)S(1)}, s32[64]{0:T(128)}, u32[]{:S(2)}) copy-start(s32[64]{0:T(128)} %param.28) | copy-start | bytes 772
  18.5 24.6 %all-to-all-start.1 = ((bf16[8,64,512]{2,0,1:T(8,128)(2,1)}), bf16[8,64,512]{2,0,1:T(8,128)(2,1)S(1)}, u32[]{:S(2)}, u32[]{:S(2)}) async-start(bf16[8,64,512]{2,0,1:T(8,128)(2,1)} %copy.75), calls=%async_computation.1 | async-start | bytes 1048576 | tf_op jit(solution)/shard_map/all_to_all | solution.py:111
  27.1 4.5 %copy-start.9 = (bf16[3,1,128,64]{2,3,1,0:T(8,128)(2,1)S(1)}, bf16[3,1,128,64]{2,3,1,0:T(8,128)(2,1)}, u32[]{:S(2)}) copy-start(bf16[3,1,128,64]{2,3,1,0:T(8,128)(2,1)} %param.32) | copy-start | bytes 147460
  31.6 1.5 copy-start.1
  43.1 70.1 %all-to-all-start = ((bf16[16,136,640]{2,1,0:T(8,128)(2,1)}), bf16[16,136,640]{2,1,0:T(8,128)(2,1)}, u32[]{:S(2)}, u32[]{:S(2)}) async-start(bf16[16,136,640]{2,1,0:T(8,128)(2,1)} %copy.72), calls=%async_computation | async-start | bytes 5570560 | tf_op jit(solution)/shard_map/all_to_all | solution.py:73
  50.1 71.1 %all-gather.5.cloned.1.call-start = ((), (), s32[]{:S(2)}) async-start(), calls=%async_computation.6 | async-start | bytes 2228224 | tf_op jit(solution)/shard_map/all_gather | solution.py:118
  124.2 1.3 copy-start.3
  125.5 2.1 collective-permute-start
  126.0 26.9 %copy-start.8 = (bf16[64,448]{1,0:T(8,128)(2,1)S(1)}, bf16[64,448]{1,0:T(8,128)(2,1)}, u32[]{:S(2)}) copy-start(bf16[64,448]{1,0:T(8,128)(2,1)} %param.24) | copy-start | bytes 172036
  152.8 9.2 %copy-start.13 = (bf16[7168]{0:T(1024)(128)(2,1)S(1)}, bf16[7168]{0:T(1024)(128)(2,1)}, u32[]{:S(2)}) copy-start(bf16[7168]{0:T(1024)(128)(2,1)} %param.25) | copy-start | bytes 43012
  152.9 0.6 copy-start.6
  154.6 22.2 %all-to-all-start.3 = ((bf16[16,64,448]{2,1,0:T(8,128)(2,1)}), bf16[16,64,448]{2,1,0:T(8,128)(2,1)}, u32[]{:S(2)}, u32[]{:S(2)}) async-start(bf16[16,64,448]{2,1,0:T(8,128)(2,1)} %broadcast_in_dim.39), calls=%async_computation.3 | async-start | bytes 2097152 | tf_op jit(solution)/shard_map/all_to_all | solution.py:140
  161.7 78.2 %all-gather.7.cloned.1.call-start = ((), (), s32[]{:S(2)}) async-start(), calls=%async_computation.7 | async-start | bytes 9748480 | tf_op jit(solution)/shard_map/all_gather | solution.py:147
  186.7 104.0 %all-gather.9.cloned.1.call-start = ((), (), s32[]{:S(2)}) async-start(), calls=%async_computation.8 | async-start | bytes 2785280 | tf_op jit(solution)/shard_map/all_gather | solution.py:152
  239.9 6.8 %copy-start.16 = (bf16[640,7168]{1,0:T(8,128)(2,1)S(1)}, bf16[640,7168]{1,0:T(8,128)(2,1)}, u32[]{:S(2)}) copy-start(bf16[640,7168]{1,0:T(8,128)(2,1)} %all-gather.7.cloned.1.call-done) | copy-start | bytes 27525124
  239.9 7.2 %copy-start.18 = (bf16[1,7168,128]{2,1,0:T(8,128)(2,1)S(1)}, bf16[1,7168,128]{2,1,0:T(8,128)(2,1)}, u32[]{:S(2)}) copy-start(bf16[1,7168,128]{2,1,0:T(8,128)(2,1)} %param.30) | copy-start | bytes 5505028
  247.2 43.6 %copy-start.4 = (bf16[2048,192]{0,1:T(8,128)(2,1)S(1)}, bf16[2048,192]{0,1:T(8,128)(2,1)}, u32[]{:S(2)}) copy-start(bf16[2048,192]{0,1:T(8,128)(2,1)} %copy.73) | copy-start | bytes 2359300
  290.8 3.8 %copy-start.2 = (bf16[2048,448]{1,0:T(8,128)(2,1)S(1)}, bf16[2048,448]{1,0:T(8,128)(2,1)}, u32[]{:S(2)}) copy-start(bf16[2048,448]{1,0:T(8,128)(2,1)} %slice.41) | copy-start | bytes 5505028
  290.8 3.8 %copy-start.17 = (bf16[10240,128]{1,0:T(8,128)(2,1)S(1)}, bf16[10240,128]{1,0:T(8,128)(2,1)}, u32[]{:S(2)}) copy-start(bf16[10240,128]{1,0:T(8,128)(2,1)} %all-gather.9.cloned.1.call-done) | copy-start | bytes 7864324
  297.0 32.7 %copy-start.12 = (s32[64,8]{0,1:T(8,128)S(1)}, s32[64,8]{0,1:T(8,128)}, u32[]{:S(2)}) copy-start(s32[64,8]{0,1:T(8,128)} %param.26) | copy-start | bytes 6148
  297.0 32.7 %copy-start.14 = (f32[64,8]{0,1:T(8,128)S(1)}, f32[64,8]{0,1:T(8,128)}, u32[]{:S(2)}) copy-start(f32[64,8]{0,1:T(8,128)} %param.27) | copy-start | bytes 6148
  297.0 44.9 %copy-start.7 = (bf16[64,448]{1,0:T(8,128)(2,1)S(1)}, bf16[64,448]{1,0:T(8,128)(2,1)}, u32[]{:S(2)}) copy-start(bf16[64,448]{1,0:T(8,128)(2,1)} %copy-done.6) | copy-start | bytes 172036
  322.9 19.0 %all-to-all-start.5 = ((bf16[16,40,448]{2,1,0:T(8,128)(2,1)}), bf16[16,40,448]{2,1,0:T(8,128)(2,1)S(1)}, u32[]{:S(2)}, u32[]{:S(2)}) async-start(bf16[16,40,448]{2,1,0:T(8,128)(2,1)} %all_to_all.44), calls=%async_computation.5 | async-start | bytes 1310720 | tf_op jit(solution)/shard_map/all_to_all | solution.py:166
Sparse Core Ops, SparseCore 0:
  53.3 51.1 all-gather.4
  186.8 53.0 all-gather.6
  250.5 40.1 all-gather.8
